TPU v7x, 256 devices: a whole 4x4x8 slice. The times are simulated.
256 devices in a mesh: seq: 64 (over z, x, core), tp: 4 (over y).
Axes of the slice: x: 4, y: 4, z: 8, core: 2. Of those that a mesh axis runs over, the one named last changes fastest.
Arguments:
- hidden: bfloat16 [8192, 1024], P('seq'), may hold values from -120 to 120
- page_table: int32 [16, 256], replicated, may hold values from -1 to 2111, as said below
- cache_len: int32 [16], replicated, may hold values from 129 to 32768, as said below
- expert_ids: int32 [8192, 2], P('seq'), may hold values from 0 to 31, all different within a row; in each aligned block of 128 rows (0 to 127, 128 to 255, ...) at most 10 rows name the same one
- w_query: bfloat16 [1024, 1024], P(None, 'tp'), may hold values from -4 to 4
- w_key: bfloat16 [1024, 1024], P(None, 'tp'), may hold values from -0.1875 to 0.1875
- w_value: bfloat16 [1024, 1024], P(None, 'tp'), may hold values from -0.1875 to 0.1875
- w_out: bfloat16 [1024, 1024], P('tp'), may hold values from -0.1875 to 0.1875
- cache_k: bfloat16 [2112, 128, 1024], P('seq', None, 'tp'), may hold values from -4000 to 4000
- cache_v: bfloat16 [2112, 128, 1024], P('seq', None, 'tp'), may hold values from -6 to 6
- moe_gain: float32 [1024], replicated, may hold values from 0.1 to 1.9
- router: float32 [1024, 32], replicated, may hold values from -0.1875 to 0.1875
- w_gate_up: bfloat16 [64, 2, 1024, 1408], P('seq', None, None, 'tp'), may hold values from -0.1875 to 0.1875
- w_down: bfloat16 [64, 1408, 1024], P('seq', 'tp'), may hold values from -0.109375 to 0.109375
Outputs:
- out: bfloat16 [8192, 1024], P('seq', 'tp')
Inputs may be any that keep to these rules, and one draw needn't show every extreme that they name: `page_table`: row r lists the pages of request r's cache in order, ceil(cache_len[r] / 128) of them, then -1; no page number appears twice in the table. `cache_len`: half of the requests have exactly 32768 cached tokens; the others have at most 384. `expert_ids`: A token names 2 different experts; among the 128 tokens of one device no expert is named more than 10 times, and on some device one expert is named exactly 10 times.
All inputs are finite; a program needn't handle non-finite values.
Results may differ from a plain program's by a relative error of at most 0.0085.
Values may be sent and summed in bfloat16 or wider, within the bound.
No kernel may reach another device: no remote copies, remote signals or barrier semaphores. Data moves between devices by JAX's collectives and lax.ppermute only.
A program may use at most 128 MiB of HBM per device.

v0:
```python
import jax
import jax.numpy as jnp
from jax import lax
from jax.sharding import PartitionSpec as P

DH = 64
EXPERTS = 32
TOP = 2
PAGE = 128
MAXP = 256
SPAN_DEVS = 4
CAP = 10


NEGATIVE = -1e30


def passed_along(value, axis, steps):
    count = lax.axis_size(axis)
    pairs = [(source, (source + steps) % count) for source in range(count)]
    return lax.ppermute(value, axis, pairs)


def rms_rows(values):
    return values * lax.rsqrt(jnp.mean(values * values, axis=-1, keepdims=True) + 1e-06)


def online_update(state, queries, keys, values, mask):
    m_old, l_old, accum = state
    scale = queries.shape[2] ** (-0.5)
    scores = jnp.einsum("nhd,khd->hnk", queries, keys, preferred_element_type=jnp.float32) * scale
    scores = jnp.where(mask[None], scores, NEGATIVE)
    m_new = jnp.maximum(m_old, jnp.max(scores, axis=-1).T)
    probs = jnp.where(mask[None], jnp.exp(scores - m_new.T[:, :, None]), 0.0)
    factor = jnp.exp(m_old - m_new)
    l_new = l_old * factor + jnp.sum(probs, axis=-1).T
    weighted = jnp.einsum(
        "hnk,khd->nhd", probs.astype(jnp.bfloat16), values, preferred_element_type=jnp.float32
    )
    return (m_new, l_new, accum * factor[:, :, None] + weighted)


def shards(
    hidden,
    page_table,
    cache_len,
    expert_ids,
    w_query,
    w_key,
    w_value,
    w_out,
    cache_k,
    cache_v,
    moe_gain,
    router,
    w_gate_up,
    w_down,
):
    tok_rows = hidden.shape[0]
    span_rows = tok_rows * SPAN_DEVS
    seq_count = lax.axis_size("seq")
    seq_index = lax.axis_index("seq")
    local_heads = w_query.shape[1] // DH
    request_total = page_table.shape[0]
    normed = rms_rows(hidden.astype(jnp.float32)).astype(jnp.bfloat16)
    queries = jnp.dot(normed, w_query, preferred_element_type=jnp.float32).astype(jnp.bfloat16)
    new_keys = (
        jnp.dot(normed, w_key, preferred_element_type=jnp.float32)
        .astype(jnp.bfloat16)
        .reshape(tok_rows, local_heads, DH)
    )
    new_values = (
        jnp.dot(normed, w_value, preferred_element_type=jnp.float32)
        .astype(jnp.bfloat16)
        .reshape(tok_rows, local_heads, DH)
    )
    page_count = cache_k.shape[0]
    page_ids = seq_index * page_count + jnp.arange(page_count, dtype=jnp.int32)
    listing = page_table.reshape(-1)
    matches = listing[None, :] == page_ids[:, None]
    entry_index = jnp.arange(listing.shape[0], dtype=jnp.int32)
    found = jnp.sum(jnp.where(matches, entry_index[None, :] + 1, 0), axis=1) - 1
    page_owner = jnp.where(found >= 0, found // MAXP, -1)
    page_order = jnp.where(found >= 0, found % MAXP, 0)
    page_limit = jnp.where(found >= 0, cache_len[jnp.maximum(page_owner, 0)], 0)
    own_request = seq_index * tok_rows // span_rows
    own_offset = seq_index * tok_rows % span_rows
    slot_range = jnp.arange(PAGE, dtype=jnp.int32)
    fresh_positions = own_offset + jnp.arange(tok_rows, dtype=jnp.int32)
    group_pages = min(4, page_count)
    owner_key = jnp.where(page_owner >= 0, page_owner, request_total)
    sort_order = jnp.argsort(owner_key, stable=True)
    filler = jnp.zeros((group_pages,) + cache_k.shape[1:], cache_k.dtype)
    sorted_k = jnp.concatenate([cache_k[sort_order], filler], axis=0)
    sorted_v = jnp.concatenate([cache_v[sort_order], filler], axis=0)
    index_filler = jnp.zeros((group_pages,), jnp.int32)
    sorted_order = jnp.concatenate([page_order[sort_order], index_filler], axis=0)
    sorted_limit = jnp.concatenate([page_limit[sort_order], index_filler], axis=0)
    group_range = jnp.arange(group_pages, dtype=jnp.int32)

    def cache_pass(state, rows, request):
        first = jnp.sum((owner_key < request).astype(jnp.int32))
        count = jnp.sum((owner_key == request).astype(jnp.int32))
        turns = (count + group_pages - 1) // group_pages

        def group_turn(turn, current):
            begin = first + turn * group_pages
            keys = lax.dynamic_slice_in_dim(sorted_k, begin, group_pages, 0).reshape(
                group_pages * PAGE, local_heads, DH
            )
            values = lax.dynamic_slice_in_dim(sorted_v, begin, group_pages, 0).reshape(
                group_pages * PAGE, local_heads, DH
            )
            orders = lax.dynamic_slice_in_dim(sorted_order, begin, group_pages, 0)
            limits = lax.dynamic_slice_in_dim(sorted_limit, begin, group_pages, 0)
            inside = turn * group_pages + group_range < count
            valid = inside[:, None] & (
                orders[:, None] * PAGE + slot_range[None, :] < limits[:, None]
            )
            mask = jnp.broadcast_to(valid.reshape(1, -1), (rows.shape[0], group_pages * PAGE))
            return online_update(current, rows, keys, values, mask)

        return lax.fori_loop(0, turns, group_turn, state)

    everyone = lax.all_gather(queries, "seq", axis=0, tiled=True)

    def visit(step, carry):
        m_run, l_run, acc_run = carry
        source = (seq_index - step) % seq_count
        request = source * tok_rows // span_rows
        positions = source * tok_rows % span_rows + jnp.arange(tok_rows, dtype=jnp.int32)
        block = lax.dynamic_slice_in_dim(everyone, source * tok_rows, tok_rows, 0).reshape(
            tok_rows, local_heads, DH
        )
        state = (m_run, l_run, acc_run.reshape(tok_rows, local_heads, DH))
        state = cache_pass(state, block, request)
        fresh_mask = (own_request == request) & (fresh_positions[None, :] <= positions[:, None])
        state = online_update(state, block, new_keys, new_values, fresh_mask)
        return passed_along((state[0], state[1], state[2].reshape(tok_rows, -1)), "seq", 1)

    start_state = (
        jnp.full((tok_rows, local_heads), NEGATIVE, jnp.float32),
        jnp.zeros((tok_rows, local_heads), jnp.float32),
        jnp.zeros((tok_rows, local_heads * DH), jnp.float32),
    )
    m_fin, l_fin, acc_fin = lax.fori_loop(0, seq_count, visit, start_state)
    attention = (
        (acc_fin.reshape(tok_rows, local_heads, DH) / l_fin[:, :, None])
        .reshape(tok_rows, -1)
        .astype(jnp.bfloat16)
    )
    head_terms = jnp.dot(attention, w_out, preferred_element_type=jnp.float32)
    mid = hidden.astype(jnp.float32) + lax.psum(head_terms.astype(jnp.bfloat16), "tp").astype(
        jnp.float32
    )
    moe_in = (rms_rows(mid) * moe_gain).astype(jnp.bfloat16)
    logits = jnp.dot(moe_in.astype(jnp.float32), router, precision=lax.Precision.HIGHEST)
    chosen = jax.nn.sigmoid(jnp.take_along_axis(logits, expert_ids, axis=1))
    gates = chosen / jnp.sum(chosen, axis=1, keepdims=True)
    flat_ids = expert_ids.reshape(-1)
    onehot = (flat_ids[:, None] == jnp.arange(EXPERTS, dtype=jnp.int32)[None, :]).astype(jnp.int32)
    ranks = jnp.sum((jnp.cumsum(onehot, axis=0) - 1) * onehot, axis=1)
    target = (flat_ids * CAP + ranks).reshape(tok_rows, TOP)
    hits = target[:, :, None] == jnp.arange(EXPERTS * CAP, dtype=jnp.int32)[None, None, :]
    placing = jnp.any(hits, axis=1).astype(jnp.bfloat16)
    combining = jnp.sum(jnp.where(hits, gates[:, :, None], 0.0), axis=1)
    packed = jnp.einsum("te,td->ed", placing, moe_in, preferred_element_type=jnp.float32).astype(
        jnp.bfloat16
    )
    width = moe_in.shape[1]
    splits = max(1, seq_count // EXPERTS)
    per_device = w_gate_up.shape[0]
    outgoing = jnp.repeat(packed.reshape(EXPERTS, CAP, width), splits, axis=0).reshape(
        seq_count, per_device, CAP, width
    )
    received = lax.all_to_all(outgoing, "seq", split_axis=0, concat_axis=0, tiled=True)
    count = received.shape[2]
    rows = received[:, 0].reshape(-1, width)
    gate = jnp.dot(rows, w_gate_up[0, 0], preferred_element_type=jnp.float32)
    upper = jnp.dot(rows, w_gate_up[0, 1], preferred_element_type=jnp.float32)
    inner = (jax.nn.gelu(gate, approximate=True) * upper).astype(jnp.bfloat16)
    results = [
        jnp.dot(inner, w_down[0], preferred_element_type=jnp.float32).reshape(
            seq_count, count, width
        )
    ]
    produced = jnp.stack(results, axis=1)
    returned = lax.all_to_all(
        produced.astype(jnp.bfloat16), "seq", split_axis=0, concat_axis=0, tiled=True
    ).astype(produced.dtype)
    columns = returned.shape[3]
    folded = jnp.sum(returned.reshape(EXPERTS, splits, CAP, columns), axis=1).reshape(
        EXPERTS * CAP, columns
    )
    mixture = jnp.dot(combining, folded, precision=lax.Precision.HIGHEST)
    tp_width = width // lax.axis_size("tp")
    mid_part = lax.dynamic_slice_in_dim(mid, lax.axis_index("tp") * tp_width, tp_width, 1)
    moe_part = lax.psum_scatter(
        mixture.astype(jnp.bfloat16), "tp", scatter_dimension=1, tiled=True
    ).astype(jnp.float32)
    return (mid_part + moe_part).astype(jnp.bfloat16)


def solution(mesh):
    in_specs = (
        P("seq", None),
        P(),
        P(),
        P("seq", None),
        P(None, "tp"),
        P(None, "tp"),
        P(None, "tp"),
        P("tp", None),
        P("seq", None, "tp"),
        P("seq", None, "tp"),
        P(),
        P(),
        P("seq", None, None, "tp"),
        P("seq", "tp", None),
    )
    out_specs = P("seq", "tp")
    return jax.shard_map(shards, mesh=mesh, in_specs=in_specs, out_specs=out_specs, check_vma=False)
```

profile of v0, /device:TPU:1, one launch (start us, length us, event | category | flops | bytes accessed | tf_op | source)
XLA Modules:
  0.0 2308.2 jit_solution(1800387318900237746)
XLA Ops:
  44.6 48.7 %all-gather.2.cloned.1.call-done = bf16[8192,256]{1,0:T(8,128)(2,1)} async-done(((bf16[128,256]{1,0:T(8,128)(2,1)}), bf16[8192,256]{1,0:T(8,128)(2,1)}) %all-gather.2.cloned.1.call-update) | async-done | bytes 4194320 | tf_op jit(solution)/shard_map/all_gather | solution.py:125
  94.6 1921.7 %while.94 = (s32[]{:T(128)}, f32[128,4]{0,1:T(4,128)S(1)}, f32[128,4]{0,1:T(4,128)}, f32[128,256]{0,1:T(8,128)}, s32[]{:T(128)}, /*index=5*/s32[33]{0:T(128)}, b...) while((s32[]{:T(128)}, f32[128,4]{0,1:T(4,128)S(1)}, ...), condition=%wide.region_12.13_spmd.clone, body=%wide.region_3.12_spmd.clone.sunk | while | flops 87003136 | bytes 8301197 | solution.py:146
  98.7 22.0 while.95
  130.5 22.0 while.95
  226.7 24.0 %collective-permute-start = (f32[128,4]{0,1:T(4,128)S(1)}, f32[128,4]{0,1:T(4,128)S(1)}, u32[]{:S(2)}, u32[]{:S(2)}) collective-permute-start(f32[128,4]{0,1:T(4,128)S(1)} %bitcast_maximum_fusion.4), channel_id=1, source_target_pairs={{0,4},{4,8},{8,12},{12,16},{16,20},{20,24},{24,28},{28,32},{32,36}... | collective-permute-start | bytes 6152 | tf_op jit(solution)/shard_map/while/body/eval_jaxpr/ppermute | solution.py:21
  318.1 21.0 collective-permute-start
  825.4 15.4 collective-permute-done.1
  859.9 18.6 collective-permute-done.1
  907.1 24.6 %collective-permute-start.2 = (f32[128,256]{0,1:T(8,128)S(1)}, f32[128,256]{0,1:T(8,128)}, u32[]{:S(2)}, u32[]{:S(2)}) collective-permute-start(f32[128,256]{0,1:T(8,128)S(1)} %bitcast.142), channel_id=1, source_target_pairs={{0,4},{4,8},{8,12},{12,16},{16,20},{20,24},{24,28},{28,32},{32,36}... | collective-permute-start | bytes 393224 | tf_op jit(solution)/shard_map/while/body/eval_jaxpr/ppermute | solution.py:21
  1034.4 21.8 collective-permute-start.1
  1187.4 23.6 %collective-permute-start = (f32[128,4]{0,1:T(4,128)S(1)}, f32[128,4]{0,1:T(4,128)S(1)}, u32[]{:S(2)}, u32[]{:S(2)}) collective-permute-start(f32[128,4]{0,1:T(4,128)S(1)} %bitcast_maximum_fusion.4), channel_id=1, source_target_pairs={{0,4},{4,8},{8,12},{12,16},{16,20},{20,24},{24,28},{28,32},{32,36}... | collective-permute-start | bytes 6152 | tf_op jit(solution)/shard_map/while/body/eval_jaxpr/ppermute | solution.py:21
  1388.3 15.5 collective-permute-start.2
  1425.5 14.8 collective-permute-start.2
  1450.9 24.4 %collective-permute-start.2 = (f32[128,256]{0,1:T(8,128)S(1)}, f32[128,256]{0,1:T(8,128)}, u32[]{:S(2)}, u32[]{:S(2)}) collective-permute-start(f32[128,256]{0,1:T(8,128)S(1)} %bitcast.142), channel_id=1, source_target_pairs={{0,4},{4,8},{8,12},{12,16},{16,20},{20,24},{24,28},{28,32},{32,36}... | collective-permute-start | bytes 393224 | tf_op jit(solution)/shard_map/while/body/eval_jaxpr/ppermute | solution.py:21
  1487.6 19.0 collective-permute-start.1
  1559.3 22.0 while.95
  1597.0 22.0 while.95
  1634.7 22.0 while.95
  1672.3 22.0 while.95
  1704.2 22.0 while.95
  1736.0 22.0 while.95
  1767.8 22.0 while.95
  1807.4 22.0 while.95
  1846.7 21.5 collective-permute-start.1
  1881.0 21.5 collective-permute-start.1
  1915.5 24.0 %collective-permute-start = (f32[128,4]{0,1:T(4,128)S(1)}, f32[128,4]{0,1:T(4,128)S(1)}, u32[]{:S(2)}, u32[]{:S(2)}) collective-permute-start(f32[128,4]{0,1:T(4,128)S(1)} %bitcast_maximum_fusion.4), channel_id=1, source_target_pairs={{0,4},{4,8},{8,12},{12,16},{16,20},{20,24},{24,28},{28,32},{32,36}... | collective-permute-start | bytes 6152 | tf_op jit(solution)/shard_map/while/body/eval_jaxpr/ppermute | solution.py:21
  1956.7 22.0 while.95
  1988.5 22.0 while.95
  2020.0 115.8 %all-reduce.6.cloned.1.call-done = bf16[128,1024]{1,0:T(8,128)(2,1)} async-done(((bf16[128,1024]{1,0:T(8,128)(2,1)}), bf16[128,1024]{1,0:T(8,128)(2,1)}) %all-reduce.6.cloned.1.call-update) | async-done | bytes 262160 | tf_op jit(solution)/shard_map/psum | solution.py:153
  2141.5 62.4 %all_to_all.10 = bf16[64,1,10,1024]{3,2,1,0:T(8,128)(2,1)} all-to-all(bf16[64,1,10,1024]{3,2,1,0:T(8,128)(2,1)S(1)} %bitcast.141), channel_id=1, replica_groups=mesh['seq'=64,'tp'=4] {'seq'}, dimensions={0} | all-to-all | bytes 2621440 | tf_op jit(solution)/shard_map/all_to_all | solution.py:176
  2228.2 45.9 %all-to-all-done.1 = bf16[64,1,10,1024]{3,2,1,0:T(8,128)(2,1)} async-done(((bf16[64,1,10,1024]{3,2,1,0:T(8,128)(2,1)}), bf16[64,1,10,1024]{3,2,1,0:T(8,128)(2,1)}, u32[]{:S(2)}, u32[]{:S(2)}) %all-to-all-start.1) | async-done | bytes 1310752 | tf_op jit(solution)/shard_map/all_to_all | solution.py:188
  2282.1 18.1 reduce-scatter.2.cloned.1.call-done
  (2170 shorter events, 1858.8 us)
Async XLA Ops:
  6.5 86.8 %all-gather.2.cloned.1.call-start = ((), (), s32[]{:S(2)}) async-start(), calls=%async_computation.3 | async-start | bytes 4259840 | tf_op jit(solution)/shard_map/all_gather | solution.py:125
  9.8 2126.0 %all-reduce.6.cloned.1.call-start = ((), (), s32[]{:S(2)}) async-start(), calls=%async_computation.4 | async-start | bytes 524288 | tf_op jit(solution)/shard_map/psum | solution.py:153
  189.8 27.1 %collective-permute-start.2 = (f32[128,256]{0,1:T(8,128)S(1)}, f32[128,256]{0,1:T(8,128)}, u32[]{:S(2)}, u32[]{:S(2)}) collective-permute-start(f32[128,256]{0,1:T(8,128)S(1)} %bitcast.142), channel_id=1, source_target_pairs={{0,4},{4,8},{8,12},{12,16},{16,20},{20,24},{24,28},{28,32},{32,36}... | collective-permute-start | bytes 393224 | tf_op jit(solution)/shard_map/while/body/eval_jaxpr/ppermute | solution.py:21
  192.2 24.1 %collective-permute-start.1 = (f32[128,4]{0,1:T(4,128)S(1)}, f32[128,4]{0,1:T(4,128)S(1)}, u32[]{:S(2)}, u32[]{:S(2)}) collective-permute-start(f32[128,4]{0,1:T(4,128)S(1)} %get-tuple-element.1071), channel_id=1, source_target_pairs={{0,4},{4,8},{8,12},{12,16},{16,20},{20,24},{24,28},{28,32},{32,36}... | collective-permute-start | bytes 6152 | tf_op jit(solution)/shard_map/while/body/eval_jaxpr/ppermute | solution.py:21
  224.2 27.1 %collective-permute-start.2 = (f32[128,256]{0,1:T(8,128)S(1)}, f32[128,256]{0,1:T(8,128)}, u32[]{:S(2)}, u32[]{:S(2)}) collective-permute-start(f32[128,256]{0,1:T(8,128)S(1)} %bitcast.142), channel_id=1, source_target_pairs={{0,4},{4,8},{8,12},{12,16},{16,20},{20,24},{24,28},{28,32},{32,36}... | collective-permute-start | bytes 393224 | tf_op jit(solution)/shard_map/while/body/eval_jaxpr/ppermute | solution.py:21
  226.6 24.1 %collective-permute-start.1 = (f32[128,4]{0,1:T(4,128)S(1)}, f32[128,4]{0,1:T(4,128)S(1)}, u32[]{:S(2)}, u32[]{:S(2)}) collective-permute-start(f32[128,4]{0,1:T(4,128)S(1)} %get-tuple-element.1071), channel_id=1, source_target_pairs={{0,4},{4,8},{8,12},{12,16},{16,20},{20,24},{24,28},{28,32},{32,36}... | collective-permute-start | bytes 6152 | tf_op jit(solution)/shard_map/while/body/eval_jaxpr/ppermute | solution.py:21
  226.7 24.7 %collective-permute-start = (f32[128,4]{0,1:T(4,128)S(1)}, f32[128,4]{0,1:T(4,128)S(1)}, u32[]{:S(2)}, u32[]{:S(2)}) collective-permute-start(f32[128,4]{0,1:T(4,128)S(1)} %bitcast_maximum_fusion.4), channel_id=1, source_target_pairs={{0,4},{4,8},{8,12},{12,16},{16,20},{20,24},{24,28},{28,32},{32,36}... | collective-permute-start | bytes 6152 | tf_op jit(solution)/shard_map/while/body/eval_jaxpr/ppermute | solution.py:21
  315.3 24.6 %collective-permute-start.2 = (f32[128,256]{0,1:T(8,128)S(1)}, f32[128,256]{0,1:T(8,128)}, u32[]{:S(2)}, u32[]{:S(2)}) collective-permute-start(f32[128,256]{0,1:T(8,128)S(1)} %bitcast.142), channel_id=1, source_target_pairs={{0,4},{4,8},{8,12},{12,16},{16,20},{20,24},{24,28},{28,32},{32,36}... | collective-permute-start | bytes 393224 | tf_op jit(solution)/shard_map/while/body/eval_jaxpr/ppermute | solution.py:21
  698.1 24.3 %collective-permute-start.2 = (f32[128,256]{0,1:T(8,128)S(1)}, f32[128,256]{0,1:T(8,128)}, u32[]{:S(2)}, u32[]{:S(2)}) collective-permute-start(f32[128,256]{0,1:T(8,128)S(1)} %bitcast.142), channel_id=1, source_target_pairs={{0,4},{4,8},{8,12},{12,16},{16,20},{20,24},{24,28},{28,32},{32,36}... | collective-permute-start | bytes 393224 | tf_op jit(solution)/shard_map/while/body/eval_jaxpr/ppermute | solution.py:21
  740.6 24.9 %collective-permute-start.2 = (f32[128,256]{0,1:T(8,128)S(1)}, f32[128,256]{0,1:T(8,128)}, u32[]{:S(2)}, u32[]{:S(2)}) collective-permute-start(f32[128,256]{0,1:T(8,128)S(1)} %bitcast.142), channel_id=1, source_target_pairs={{0,4},{4,8},{8,12},{12,16},{16,20},{20,24},{24,28},{28,32},{32,36}... | collective-permute-start | bytes 393224 | tf_op jit(solution)/shard_map/while/body/eval_jaxpr/ppermute | solution.py:21
  907.1 26.6 %collective-permute-start.2 = (f32[128,256]{0,1:T(8,128)S(1)}, f32[128,256]{0,1:T(8,128)}, u32[]{:S(2)}, u32[]{:S(2)}) collective-permute-start(f32[128,256]{0,1:T(8,128)S(1)} %bitcast.142), channel_id=1, source_target_pairs={{0,4},{4,8},{8,12},{12,16},{16,20},{20,24},{24,28},{28,32},{32,36}... | collective-permute-start | bytes 393224 | tf_op jit(solution)/shard_map/while/body/eval_jaxpr/ppermute | solution.py:21
  997.7 27.1 %collective-permute-start.2 = (f32[128,256]{0,1:T(8,128)S(1)}, f32[128,256]{0,1:T(8,128)}, u32[]{:S(2)}, u32[]{:S(2)}) collective-permute-start(f32[128,256]{0,1:T(8,128)S(1)} %bitcast.142), channel_id=1, source_target_pairs={{0,4},{4,8},{8,12},{12,16},{16,20},{20,24},{24,28},{28,32},{32,36}... | collective-permute-start | bytes 393224 | tf_op jit(solution)/shard_map/while/body/eval_jaxpr/ppermute | solution.py:21
  1032.0 27.1 %collective-permute-start.2 = (f32[128,256]{0,1:T(8,128)S(1)}, f32[128,256]{0,1:T(8,128)}, u32[]{:S(2)}, u32[]{:S(2)}) collective-permute-start(f32[128,256]{0,1:T(8,128)S(1)} %bitcast.142), channel_id=1, source_target_pairs={{0,4},{4,8},{8,12},{12,16},{16,20},{20,24},{24,28},{28,32},{32,36}... | collective-permute-start | bytes 393224 | tf_op jit(solution)/shard_map/while/body/eval_jaxpr/ppermute | solution.py:21
  1034.4 24.1 %collective-permute-start.1 = (f32[128,4]{0,1:T(4,128)S(1)}, f32[128,4]{0,1:T(4,128)S(1)}, u32[]{:S(2)}, u32[]{:S(2)}) collective-permute-start(f32[128,4]{0,1:T(4,128)S(1)} %get-tuple-element.1071), channel_id=1, source_target_pairs={{0,4},{4,8},{8,12},{12,16},{16,20},{20,24},{24,28},{28,32},{32,36}... | collective-permute-start | bytes 6152 | tf_op jit(solution)/shard_map/while/body/eval_jaxpr/ppermute | solution.py:21
  1084.5 24.1 %collective-permute-start.2 = (f32[128,256]{0,1:T(8,128)S(1)}, f32[128,256]{0,1:T(8,128)}, u32[]{:S(2)}, u32[]{:S(2)}) collective-permute-start(f32[128,256]{0,1:T(8,128)S(1)} %bitcast.142), channel_id=1, source_target_pairs={{0,4},{4,8},{8,12},{12,16},{16,20},{20,24},{24,28},{28,32},{32,36}... | collective-permute-start | bytes 393224 | tf_op jit(solution)/shard_map/while/body/eval_jaxpr/ppermute | solution.py:21
  1115.9 27.1 %collective-permute-start.2 = (f32[128,256]{0,1:T(8,128)S(1)}, f32[128,256]{0,1:T(8,128)}, u32[]{:S(2)}, u32[]{:S(2)}) collective-permute-start(f32[128,256]{0,1:T(8,128)S(1)} %bitcast.142), channel_id=1, source_target_pairs={{0,4},{4,8},{8,12},{12,16},{16,20},{20,24},{24,28},{28,32},{32,36}... | collective-permute-start | bytes 393224 | tf_op jit(solution)/shard_map/while/body/eval_jaxpr/ppermute | solution.py:21
  1150.2 27.1 %collective-permute-start.2 = (f32[128,256]{0,1:T(8,128)S(1)}, f32[128,256]{0,1:T(8,128)}, u32[]{:S(2)}, u32[]{:S(2)}) collective-permute-start(f32[128,256]{0,1:T(8,128)S(1)} %bitcast.142), channel_id=1, source_target_pairs={{0,4},{4,8},{8,12},{12,16},{16,20},{20,24},{24,28},{28,32},{32,36}... | collective-permute-start | bytes 393224 | tf_op jit(solution)/shard_map/while/body/eval_jaxpr/ppermute | solution.py:21
  1152.6 24.1 %collective-permute-start.1 = (f32[128,4]{0,1:T(4,128)S(1)}, f32[128,4]{0,1:T(4,128)S(1)}, u32[]{:S(2)}, u32[]{:S(2)}) collective-permute-start(f32[128,4]{0,1:T(4,128)S(1)} %get-tuple-element.1071), channel_id=1, source_target_pairs={{0,4},{4,8},{8,12},{12,16},{16,20},{20,24},{24,28},{28,32},{32,36}... | collective-permute-start | bytes 6152 | tf_op jit(solution)/shard_map/while/body/eval_jaxpr/ppermute | solution.py:21
  1184.6 27.1 %collective-permute-start.2 = (f32[128,256]{0,1:T(8,128)S(1)}, f32[128,256]{0,1:T(8,128)}, u32[]{:S(2)}, u32[]{:S(2)}) collective-permute-start(f32[128,256]{0,1:T(8,128)S(1)} %bitcast.142), channel_id=1, source_target_pairs={{0,4},{4,8},{8,12},{12,16},{16,20},{20,24},{24,28},{28,32},{32,36}... | collective-permute-start | bytes 393224 | tf_op jit(solution)/shard_map/while/body/eval_jaxpr/ppermute | solution.py:21
  1186.9 24.1 %collective-permute-start.1 = (f32[128,4]{0,1:T(4,128)S(1)}, f32[128,4]{0,1:T(4,128)S(1)}, u32[]{:S(2)}, u32[]{:S(2)}) collective-permute-start(f32[128,4]{0,1:T(4,128)S(1)} %get-tuple-element.1071), channel_id=1, source_target_pairs={{0,4},{4,8},{8,12},{12,16},{16,20},{20,24},{24,28},{28,32},{32,36}... | collective-permute-start | bytes 6152 | tf_op jit(solution)/shard_map/while/body/eval_jaxpr/ppermute | solution.py:21
  1187.4 24.3 %collective-permute-start = (f32[128,4]{0,1:T(4,128)S(1)}, f32[128,4]{0,1:T(4,128)S(1)}, u32[]{:S(2)}, u32[]{:S(2)}) collective-permute-start(f32[128,4]{0,1:T(4,128)S(1)} %bitcast_maximum_fusion.4), channel_id=1, source_target_pairs={{0,4},{4,8},{8,12},{12,16},{16,20},{20,24},{24,28},{28,32},{32,36}... | collective-permute-start | bytes 6152 | tf_op jit(solution)/shard_map/while/body/eval_jaxpr/ppermute | solution.py:21
  1450.9 26.3 %collective-permute-start.2 = (f32[128,256]{0,1:T(8,128)S(1)}, f32[128,256]{0,1:T(8,128)}, u32[]{:S(2)}, u32[]{:S(2)}) collective-permute-start(f32[128,256]{0,1:T(8,128)S(1)} %bitcast.142), channel_id=1, source_target_pairs={{0,4},{4,8},{8,12},{12,16},{16,20},{20,24},{24,28},{28,32},{32,36}... | collective-permute-start | bytes 393224 | tf_op jit(solution)/shard_map/while/body/eval_jaxpr/ppermute | solution.py:21
  1485.0 22.8 collective-permute-start.2
  1844.3 27.1 %collective-permute-start.2 = (f32[128,256]{0,1:T(8,128)S(1)}, f32[128,256]{0,1:T(8,128)}, u32[]{:S(2)}, u32[]{:S(2)}) collective-permute-start(f32[128,256]{0,1:T(8,128)S(1)} %bitcast.142), channel_id=1, source_target_pairs={{0,4},{4,8},{8,12},{12,16},{16,20},{20,24},{24,28},{28,32},{32,36}... | collective-permute-start | bytes 393224 | tf_op jit(solution)/shard_map/while/body/eval_jaxpr/ppermute | solution.py:21
  1846.7 24.1 %collective-permute-start.1 = (f32[128,4]{0,1:T(4,128)S(1)}, f32[128,4]{0,1:T(4,128)S(1)}, u32[]{:S(2)}, u32[]{:S(2)}) collective-permute-start(f32[128,4]{0,1:T(4,128)S(1)} %get-tuple-element.1071), channel_id=1, source_target_pairs={{0,4},{4,8},{8,12},{12,16},{16,20},{20,24},{24,28},{28,32},{32,36}... | collective-permute-start | bytes 6152 | tf_op jit(solution)/shard_map/while/body/eval_jaxpr/ppermute | solution.py:21
  1878.7 27.1 %collective-permute-start.2 = (f32[128,256]{0,1:T(8,128)S(1)}, f32[128,256]{0,1:T(8,128)}, u32[]{:S(2)}, u32[]{:S(2)}) collective-permute-start(f32[128,256]{0,1:T(8,128)S(1)} %bitcast.142), channel_id=1, source_target_pairs={{0,4},{4,8},{8,12},{12,16},{16,20},{20,24},{24,28},{28,32},{32,36}... | collective-permute-start | bytes 393224 | tf_op jit(solution)/shard_map/while/body/eval_jaxpr/ppermute | solution.py:21
  1881.0 24.1 %collective-permute-start.1 = (f32[128,4]{0,1:T(4,128)S(1)}, f32[128,4]{0,1:T(4,128)S(1)}, u32[]{:S(2)}, u32[]{:S(2)}) collective-permute-start(f32[128,4]{0,1:T(4,128)S(1)} %get-tuple-element.1071), channel_id=1, source_target_pairs={{0,4},{4,8},{8,12},{12,16},{16,20},{20,24},{24,28},{28,32},{32,36}... | collective-permute-start | bytes 6152 | tf_op jit(solution)/shard_map/while/body/eval_jaxpr/ppermute | solution.py:21
  1913.0 27.1 %collective-permute-start.2 = (f32[128,256]{0,1:T(8,128)S(1)}, f32[128,256]{0,1:T(8,128)}, u32[]{:S(2)}, u32[]{:S(2)}) collective-permute-start(f32[128,256]{0,1:T(8,128)S(1)} %bitcast.142), channel_id=1, source_target_pairs={{0,4},{4,8},{8,12},{12,16},{16,20},{20,24},{24,28},{28,32},{32,36}... | collective-permute-start | bytes 393224 | tf_op jit(solution)/shard_map/while/body/eval_jaxpr/ppermute | solution.py:21
  1915.4 24.1 %collective-permute-start.1 = (f32[128,4]{0,1:T(4,128)S(1)}, f32[128,4]{0,1:T(4,128)S(1)}, u32[]{:S(2)}, u32[]{:S(2)}) collective-permute-start(f32[128,4]{0,1:T(4,128)S(1)} %get-tuple-element.1071), channel_id=1, source_target_pairs={{0,4},{4,8},{8,12},{12,16},{16,20},{20,24},{24,28},{28,32},{32,36}... | collective-permute-start | bytes 6152 | tf_op jit(solution)/shard_map/while/body/eval_jaxpr/ppermute | solution.py:21
  1915.5 24.7 %collective-permute-start = (f32[128,4]{0,1:T(4,128)S(1)}, f32[128,4]{0,1:T(4,128)S(1)}, u32[]{:S(2)}, u32[]{:S(2)}) collective-permute-start(f32[128,4]{0,1:T(4,128)S(1)} %bitcast_maximum_fusion.4), channel_id=1, source_target_pairs={{0,4},{4,8},{8,12},{12,16},{16,20},{20,24},{24,28},{28,32},{32,36}... | collective-permute-start | bytes 6152 | tf_op jit(solution)/shard_map/while/body/eval_jaxpr/ppermute | solution.py:21
  2217.2 56.9 %all-to-all-start.1 = ((bf16[64,1,10,1024]{3,2,1,0:T(8,128)(2,1)}), bf16[64,1,10,1024]{3,2,1,0:T(8,128)(2,1)}, u32[]{:S(2)}, u32[]{:S(2)}) async-start(bf16[64,1,10,1024]{3,2,1,0:T(8,128)(2,1)} %copy.103), calls=%async_computation.1 | async-start | bytes 4194304 | tf_op jit(solution)/shard_map/all_to_all | solution.py:188
  2224.5 75.6 %reduce-scatter.2.cloned.1.call-start = ((), (), s32[]{:S(2)}) async-start(), calls=%async_computation.5 | async-start | bytes 327680 | tf_op jit(solution)/shard_map/reduce_scatter | solution.py:198
  (328 other events, 1699.0 us)
Sparse Core Ops, SparseCore 0:
  10.1 83.1 all-gather.1
  2019.3 116.4 all-reduce.5
  2282.2 17.9 reduce-scatter.1
where the time goes:
time: 2330 us; the launch traced here: 2310 us
  starting transfers between devices  822 us (35%)
  local copies, waits for them, and re-layouts  416 us (18%)
  waiting for transfers between devices  374 us (16%)
  other arithmetic  288 us (12%)
  matrix products  258 us (11%)
  loops' own time  75.6 us (3%)
  blocking collectives  62.4 us (3%)
    ppermute x192, starting transfers between devices, passed_along(): return lax.ppermute(value, axis, pairs)  814 us
    dot_general x108, matrix products, online_update(): jnp.einsum('hnk,khd->nhd', probs.astype(jnp.bfloat16), values, preferred_...  155 us
    ppermute x192, waiting for transfers between devices, passed_along(): return lax.ppermute(value, axis, pairs)  145 us
    dynamic_slice x44, local copies, waits for them, and re-layouts, group_turn(): lax.dynamic_slice_in_dim(sorted_v, begin, group_pages, 0)  116 us
    psum x1, waiting for transfers between devices, shards(): lax.psum(head_terms.astype(jnp.bfloat16), 'tp').astype(jnp.float32)  116 us
    reduce_sum x64, other arithmetic, cache_pass(): first = jnp.sum((owner_key < request).astype(jnp.int32))  87.5 us
    dot_general x108, matrix products, online_update(): jnp.einsum('nhd,khd->hnk', queries, keys, preferred_element_type=jnp.floa...  87.5 us
    all_to_all x1, blocking collectives, shards(): lax.all_to_all(outgoing, 'seq', split_axis=0, concat_axis=0, tiled=True)  62.4 us
  transfers between devices with their start and end apart: 196, of which 73 were waited for; matrix products, arithmetic and copies ran while one was open for 2% of the time, Pallas kernels for 0%

commit v1 on v0

--- a/solution.py
+++ b/solution.py
@@ -86,69 +86,59 @@
     own_request = seq_index * tok_rows // span_rows
     own_offset = seq_index * tok_rows % span_rows
     slot_range = jnp.arange(PAGE, dtype=jnp.int32)
-    fresh_positions = own_offset + jnp.arange(tok_rows, dtype=jnp.int32)
-    group_pages = min(4, page_count)
-    owner_key = jnp.where(page_owner >= 0, page_owner, request_total)
-    sort_order = jnp.argsort(owner_key, stable=True)
-    filler = jnp.zeros((group_pages,) + cache_k.shape[1:], cache_k.dtype)
-    sorted_k = jnp.concatenate([cache_k[sort_order], filler], axis=0)
-    sorted_v = jnp.concatenate([cache_v[sort_order], filler], axis=0)
-    index_filler = jnp.zeros((group_pages,), jnp.int32)
-    sorted_order = jnp.concatenate([page_order[sort_order], index_filler], axis=0)
-    sorted_limit = jnp.concatenate([page_limit[sort_order], index_filler], axis=0)
-    group_range = jnp.arange(group_pages, dtype=jnp.int32)
-
-    def cache_pass(state, rows, request):
-        first = jnp.sum((owner_key < request).astype(jnp.int32))
-        count = jnp.sum((owner_key == request).astype(jnp.int32))
-        turns = (count + group_pages - 1) // group_pages
-
-        def group_turn(turn, current):
-            begin = first + turn * group_pages
-            keys = lax.dynamic_slice_in_dim(sorted_k, begin, group_pages, 0).reshape(
-                group_pages * PAGE, local_heads, DH
-            )
-            values = lax.dynamic_slice_in_dim(sorted_v, begin, group_pages, 0).reshape(
-                group_pages * PAGE, local_heads, DH
-            )
-            orders = lax.dynamic_slice_in_dim(sorted_order, begin, group_pages, 0)
-            limits = lax.dynamic_slice_in_dim(sorted_limit, begin, group_pages, 0)
-            inside = turn * group_pages + group_range < count
-            valid = inside[:, None] & (
-                orders[:, None] * PAGE + slot_range[None, :] < limits[:, None]
-            )
-            mask = jnp.broadcast_to(valid.reshape(1, -1), (rows.shape[0], group_pages * PAGE))
-            return online_update(current, rows, keys, values, mask)
-
-        return lax.fori_loop(0, turns, group_turn, state)
-
-    everyone = lax.all_gather(queries, "seq", axis=0, tiled=True)
-
-    def visit(step, carry):
-        m_run, l_run, acc_run = carry
-        source = (seq_index - step) % seq_count
-        request = source * tok_rows // span_rows
-        positions = source * tok_rows % span_rows + jnp.arange(tok_rows, dtype=jnp.int32)
-        block = lax.dynamic_slice_in_dim(everyone, source * tok_rows, tok_rows, 0).reshape(
-            tok_rows, local_heads, DH
-        )
-        state = (m_run, l_run, acc_run.reshape(tok_rows, local_heads, DH))
-        state = cache_pass(state, block, request)
-        fresh_mask = (own_request == request) & (fresh_positions[None, :] <= positions[:, None])
-        state = online_update(state, block, new_keys, new_values, fresh_mask)
-        return passed_along((state[0], state[1], state[2].reshape(tok_rows, -1)), "seq", 1)
-
-    start_state = (
-        jnp.full((tok_rows, local_heads), NEGATIVE, jnp.float32),
-        jnp.zeros((tok_rows, local_heads), jnp.float32),
-        jnp.zeros((tok_rows, local_heads * DH), jnp.float32),
-    )
-    m_fin, l_fin, acc_fin = lax.fori_loop(0, seq_count, visit, start_state)
-    attention = (
-        (acc_fin.reshape(tok_rows, local_heads, DH) / l_fin[:, :, None])
-        .reshape(tok_rows, -1)
-        .astype(jnp.bfloat16)
-    )
+    page_valid = (found >= 0)[:, None] & (
+        page_order[:, None] * PAGE + slot_range[None, :] < page_limit[:, None]
+    )
+    span_positions = jnp.arange(span_rows, dtype=jnp.int32)
+    fresh_mask = span_positions[:, None] >= own_offset + jnp.arange(tok_rows, dtype=jnp.int32)[None, :]
+    mask = jnp.concatenate(
+        [
+            jnp.broadcast_to(page_valid[:, None, :], (page_count, span_rows, PAGE)),
+            fresh_mask[None],
+        ],
+        axis=0,
+    )
+    owners = jnp.concatenate([page_owner, own_request[None]], axis=0)
+    keys = jnp.concatenate(
+        [cache_k.reshape(page_count, PAGE, local_heads, DH), new_keys[None]], axis=0
+    )
+    values = jnp.concatenate(
+        [cache_v.reshape(page_count, PAGE, local_heads, DH), new_values[None]], axis=0
+    )
+    everyone = lax.all_gather(queries, "seq", axis=0, tiled=True).reshape(
+        request_total, span_rows, local_heads, DH
+    )
+    rows = everyone[jnp.maximum(owners, 0)]
+    scores = jnp.einsum("bqhd,bkhd->bhqk", rows, keys, preferred_element_type=jnp.float32) * (
+        DH ** (-0.5)
+    )
+    scores = jnp.where(mask[:, None], scores, NEGATIVE)
+    m_block = jnp.max(scores, axis=-1)
+    probs = jnp.where(mask[:, None], jnp.exp(scores - m_block[..., None]), 0.0)
+    l_block = jnp.sum(probs, axis=-1)
+    acc_block = jnp.einsum(
+        "bhqk,bkhd->bqhd", probs.astype(jnp.bfloat16), values, preferred_element_type=jnp.float32
+    )
+    onehot = owners[:, None] == jnp.arange(request_total, dtype=jnp.int32)[None, :]
+    m_local = jnp.max(jnp.where(onehot[:, :, None, None], m_block[:, None], NEGATIVE), axis=0)
+    m_global = lax.pmax(m_local, "seq")
+    factor = jnp.exp(m_block - m_global[jnp.maximum(owners, 0)])
+    scaled_acc = acc_block * jnp.transpose(factor, (0, 2, 1))[..., None]
+    scaled_l = jnp.transpose(l_block * factor, (0, 2, 1))
+    packed_state = jnp.concatenate(
+        [scaled_acc.reshape(owners.shape[0], span_rows, -1), scaled_l], axis=2
+    )
+    state_width = packed_state.shape[2]
+    folded_state = jnp.einsum(
+        "br,bx->rx",
+        onehot.astype(jnp.float32),
+        packed_state.reshape(owners.shape[0], -1),
+        precision=lax.Precision.HIGHEST,
+    ).reshape(request_total * span_rows, state_width)
+    own_state = lax.psum_scatter(folded_state, "seq", scatter_dimension=0, tiled=True)
+    acc_fin = own_state[:, : local_heads * DH].reshape(tok_rows, local_heads, DH)
+    l_fin = own_state[:, local_heads * DH :]
+    attention = (acc_fin / l_fin[:, :, None]).reshape(tok_rows, -1).astype(jnp.bfloat16)
     head_terms = jnp.dot(attention, w_out, preferred_element_type=jnp.float32)
     mid = hidden.astype(jnp.float32) + lax.psum(head_terms.astype(jnp.bfloat16), "tp").astype(
         jnp.float32

time: 2330 us -> 833 us (0.36)
  starting transfers between devices: 822 us -> 7.31 us
  local copies, waits for them, and re-layouts: 416 us -> 142 us
  other arithmetic: 288 us -> 48.6 us
  matrix products: 258 us -> 68.6 us
  waiting for transfers between devices: 374 us -> 488 us
  loops' own time: 75.6 us -> 0 us
    ppermute x192 -> x0, starting transfers between devices: 814 us -> none  [passed_along(): return lax.ppermute(value, axis, pairs)]
    dynamic_slice x216 -> x0, local copies, waits for them, and re-layouts: 208 us -> none  [the longest x44 116 us: group_turn(): lax.dynamic_slice_in_dim(sorted_v, begin, group_pages, 0)]
    dot_general x216 -> x3, matrix products: 243 us -> 52.2 us  [the longest x1 20 us: shards(): jnp.einsum('bhqk,bkhd->bqhd', probs.astype(jnp.bfloat16), values, preferr...]
    pmax x0 -> x1, waiting for transfers between devices: none -> 156 us  [shards(): m_global = lax.pmax(m_local, 'seq')]
    reduce_scatter x0 -> x1, waiting for transfers between devices: none -> 152 us  [shards(): lax.psum_scatter(folded_state, 'seq', scatter_dimension=0, tiled=True)]
    ppermute x192 -> x0, waiting for transfers between devices: 145 us -> none  [passed_along(): return lax.ppermute(value, axis, pairs)]
    reduce_sum x172 -> x1, other arithmetic: 101 us -> 17.6 us  [shards(): l_block = jnp.sum(probs, axis=-1)]
    another operation x65 -> x0, loops' own time: 75.6 us -> none  [the longest x1 49.4 us: shards(): m_fin, l_fin, acc_fin = lax.fori_loop(0, seq_count, visit, start_state)]
  transfers between devices with their start and end apart: 196 -> 6, of which waited for: 73 -> 6; matrix products, arithmetic and copies ran while one was open for 2% -> 5% of each run, Pallas kernels for 0% -> 0%
where the time goes in v1:
time: 833 us; the launch traced here: 830 us
  waiting for transfers between devices  488 us (59%)
  local copies, waits for them, and re-layouts  142 us (17%)
  matrix products  68.6 us (8%)
  blocking collectives  62.3 us (7%)
  other arithmetic  48.6 us (6%)
  between operations  13.5 us (2%)
    pmax x1, waiting for transfers between devices, shards(): m_global = lax.pmax(m_local, 'seq')  156 us
    reduce_scatter x1, waiting for transfers between devices, shards(): lax.psum_scatter(folded_state, 'seq', scatter_dimension=0, tiled=True)  152 us
    all_gather x1, waiting for transfers between devices, shards(): lax.all_gather(queries, 'seq', axis=0, tiled=True)  68.7 us
    all_to_all x1, blocking collectives, shards(): lax.all_to_all(outgoing, 'seq', split_axis=0, concat_axis=0, tiled=True)  62.3 us
    psum x1, waiting for transfers between devices, shards(): lax.psum(head_terms.astype(jnp.bfloat16), 'tp').astype(jnp.float32)  47.2 us
    all_to_all x1, waiting for transfers between devices, shards(): lax.all_to_all(produced.astype(jnp.bfloat16), 'seq', split_axis=0, concat...  45.8 us
    reshape x1, local copies, waits for them, and re-layouts, shards(): packed_state.reshape(owners.shape[0], -1)  39.6 us
    reshape x2, local copies, waits for them, and re-layouts, shards(): lax.all_gather(queries, 'seq', axis=0, tiled=True)  25.6 us
  transfers between devices with their start and end apart: 6, of which 6 were waited for; matrix products, arithmetic and copies ran while one was open for 5% of the time, Pallas kernels for 0%

profile of v1, /device:TPU:1, one launch (start us, length us, event | category | flops | bytes accessed | tf_op | source)
XLA Modules:
  0.0 830.0 jit_solution(9411528269376874684)
XLA Ops:
  7.8 2.0 convolution_convert_fusion.5
  12.8 4.1 copy.130
  18.9 2.4 copy.126
  24.6 68.7 %all-gather.2.cloned.1.call-done = bf16[8192,256]{1,0:T(8,128)(2,1)} async-done(((bf16[128,256]{1,0:T(8,128)(2,1)}), bf16[8192,256]{1,0:T(8,128)(2,1)}) %all-gather.2.cloned.1.call-update) | async-done | bytes 4194320 | tf_op jit(solution)/shard_map/all_gather | solution.py:108
  93.3 12.9 %reshape.377 = bf16[16,512,4,64]{3,2,1,0:T(4,128)(2,1)} reshape(bf16[8192,256]{1,0:T(8,128)(2,1)} %all-gather.2.cloned.1.call-done) | data formatting | bytes 8388608 | tf_op jit(solution)/shard_map/reshape | solution.py:108
  106.2 12.7 %copy.129 = bf16[16,512,4,64]{1,3,2,0:T(8,128)(2,1)} copy(bf16[16,512,4,64]{3,2,1,0:T(4,128)(2,1)} %reshape.377) | data formatting | bytes 8388608 | tf_op jit(solution)/shard_map/reshape | solution.py:108
  118.9 7.5 gather_fusion.1
  126.3 17.2 %fusion = (f32[34,4,512]{2,1,0:T(4,128)S(1)}, f32[34,4,512,128]{2,3,1,0:T(8,128)}) fusion(pred[34,512,128]{1,2,0:T(8,128)(4,1)S(1)} %pad_add_fusion, bf16[34,512,4,64]{1,3,2,0:T(8,128)(2,1)} %gather_fusion.1, bf16[1,128,4,64]{1,3,2,0:T(8,128)(2,1)} %bitcast.87, bf16[33,128,4,64]{1,3,2,0:T(8,128)(2,1)} %bitcast.84), kind=kOutput, calls=%fused_computation.6 | convolution fusion | flops 1168633856 | bytes 49299456 | tf_op jit(solution)/shard_map/bqhd,bkhd->bhqk/dot_general | solution.py:112
  145.0 17.6 %fusion.1 = f32[34,4,512]{2,1,0:T(4,128)} fusion(f32[34,4,512,128]{2,3,1,0:T(8,128)} %get-tuple-element.15, f32[34,4,512]{2,1,0:T(4,128)S(1)} %get-tuple-element.14, pred[34,512,128]{1,2,0:T(8,128)(4,1)S(1)} %pad_add_fusion), kind=kLoop, calls=%fused_computation.8 | loop fusion | flops 44494848 | bytes 38436864 | tf_op jit(solution)/shard_map/reduce_sum | solution.py:118
  162.6 155.5 %all-reduce.3.cloned.1.call-done = f32[16,4,512]{2,1,0:T(4,128)} async-done(((f32[16,4,512]{2,1,0:T(4,128)}), f32[16,4,512]{2,1,0:T(4,128)}) %all-reduce.3.cloned.1.call-update) | async-done | bytes 131088 | tf_op jit(solution)/shard_map/pmax | solution.py:124
  318.1 2.4 gather_fusion.2
  320.5 1.9 bitcast_multiply_fusion.1
  322.4 20.0 %bitcast_multiply_fusion = f32[34,512,4,64]{1,3,2,0:T(8,128)} fusion(f32[34,512,4]{1,2,0:T(4,128)S(1)} %get-tuple-element.8, f32[34,4,512,128]{2,3,1,0:T(8,128)} %get-tuple-element.15, f32[34,4,512]{2,1,0:T(4,128)S(1)} %get-tuple-element.14, pred[34,512,128]{1,2,0:T(8,128)(4,1)S(1)} %pad_add_fusion, bf16[1,128,4,64]{1,3,2,0:T(8,128)(2,1)} %bitcast.86, ...), kind=kOutput, calls=%fused_computation.11 | convolution fusion | flops 1190985728 | bytes 58490880 | tf_op jit(solution)/shard_map/bhqk,bkhd->bqhd/dot_general | solution.py:119
  342.4 18.4 %copy.134 = f32[34,512,256]{2,1,0:T(8,128)} copy(f32[34,512,256]{1,2,0:T(8,128)} %bitcast.80) | data formatting | bytes 35651584 | tf_op jit(solution)/shard_map/reshape | solution.py:129
  360.8 4.9 copy.135
  365.7 19.7 %pad_maximum_fusion = f32[34,512,260]{2,1,0:T(8,128)} fusion(f32[34,512,4]{2,1,0:T(8,128)} %copy.135, f32[34,512,256]{2,1,0:T(8,128)} %copy.134), kind=kLoop, calls=%fused_computation.7 | loop fusion | flops 4526080 | bytes 36208640 | tf_op jit(solution)/shard_map/concatenate | solution.py:128
  385.4 39.6 %reshape.331 = f32[34,133120]{1,0:T(8,128)} reshape(f32[34,512,260]{2,1,0:T(8,128)} %pad_maximum_fusion) | data formatting | bytes 36208640 | tf_op jit(solution)/shard_map/reshape | solution.py:135
  425.0 14.9 %fusion.54 = f32[16,133120]{1,0:T(8,128)} fusion(f32[34,133120]{1,0:T(8,128)} %reshape.331, s32[34]{0:T(128)S(1)} %pad_add_fusion.1), kind=kOutput, calls=%fused_computation.121 | convolution fusion | flops 869007872 | bytes 26624136 | tf_op jit(solution)/shard_map/br,bx->rx/dot_general | solution.py:132
  439.9 21.7 %reshape.332 = f32[8192,260]{1,0:T(8,128)} reshape(f32[16,133120]{1,0:T(8,128)} %fusion.54) | data formatting | bytes 17039360 | tf_op jit(solution)/shard_map/reshape | solution.py:137
  463.8 152.4 %reduce-scatter.3.cloned.1.call-done = f32[128,260]{1,0:T(8,128)} async-done(((f32[8192,260]{1,0:T(8,128)}), f32[128,260]{1,0:T(8,128)}) %reduce-scatter.3.cloned.1.call-update) | async-done | bytes 133136 | tf_op jit(solution)/shard_map/reduce_scatter | solution.py:138
  617.3 1.8 convolution_convert_fusion.3
  619.2 47.2 %all-reduce.5.cloned.1.call-done = bf16[128,1024]{1,0:T(8,128)(2,1)} async-done(((bf16[128,1024]{1,0:T(8,128)(2,1)}), bf16[128,1024]{1,0:T(8,128)(2,1)}) %all-reduce.5.cloned.1.call-update) | async-done | bytes 262160 | tf_op jit(solution)/shard_map/psum | solution.py:143
  666.3 1.8 convert_add_fusion
  670.1 62.3 %all_to_all.10 = bf16[64,1,10,1024]{3,2,1,0:T(8,128)(2,1)S(1)} all-to-all(bf16[64,1,10,1024]{3,2,1,0:T(8,128)(2,1)S(1)} %bitcast.82), channel_id=1, replica_groups=mesh['seq'=64,'tp'=4] {'seq'}, dimensions={0} | all-to-all | bytes 2621440 | tf_op jit(solution)/shard_map/all_to_all | solution.py:166
  733.8 2.3 fusion.30
  736.0 2.3 fusion.20
  739.7 2.1 copy.146
  741.9 7.0 all-to-all-start.1
  750.5 2.0 gather_fusion.3
  752.8 45.8 %all-to-all-done.1 = bf16[64,1,10,1024]{3,2,1,0:T(8,128)(2,1)S(1)} async-done(((bf16[64,1,10,1024]{3,2,1,0:T(8,128)(2,1)}), bf16[64,1,10,1024]{3,2,1,0:T(8,128)(2,1)S(1)}, u32[]{:S(2)}, u32[]{:S(2)}) %all-to-all-start.1) | async-done | bytes 1310752 | tf_op jit(solution)/shard_map/all_to_all | solution.py:178
  798.5 1.8 convert_reduce_fusion
  803.8 18.1 %reduce-scatter.5.cloned.1.call-done = bf16[128,256]{1,0:T(8,128)(2,1)} async-done(((bf16[128,1024]{1,0:T(8,128)(2,1)}), bf16[128,256]{1,0:T(8,128)(2,1)}) %reduce-scatter.5.cloned.1.call-update) | async-done | bytes 65552 | tf_op jit(solution)/shard_map/reduce_scatter | solution.py:188
  (91 shorter events, 25.6 us)
Async XLA Ops:
  6.5 732.3 %copy-start = (bf16[1,352,1024]{2,1,0:T(8,128)(2,1)S(1)}, bf16[1,352,1024]{2,1,0:T(8,128)(2,1)}, u32[]{:S(2)}) copy-start(bf16[1,352,1024]{2,1,0:T(8,128)(2,1)} %param.27) | copy-start | bytes 2162692
  6.5 10.4 %copy-start.2 = (bf16[128,1024]{1,0:T(8,128)(2,1)S(1)}, bf16[128,1024]{1,0:T(8,128)(2,1)}, u32[]{:S(2)}) copy-start(bf16[128,1024]{1,0:T(8,128)(2,1)} %param.14) | copy-start | bytes 786436
  6.5 12.4 %copy-start.4 = (bf16[33,128,256]{2,1,0:T(8,128)(2,1)S(1)}, bf16[33,128,256]{2,1,0:T(8,128)(2,1)}, u32[]{:S(2)}) copy-start(bf16[33,128,256]{2,1,0:T(8,128)(2,1)} %param.23) | copy-start | bytes 6488068
  6.5 86.8 %all-gather.2.cloned.1.call-start = ((), (), s32[]{:S(2)}) async-start(), calls=%async_computation.4 | async-start | bytes 4259840 | tf_op jit(solution)/shard_map/all_gather | solution.py:108
  9.8 308.3 %all-reduce.3.cloned.1.call-start = ((), (), s32[]{:S(2)}) async-start(), calls=%async_computation.5 | async-start | bytes 262144 | tf_op jit(solution)/shard_map/pmax | solution.py:124
  12.8 8.8 %copy-start.1 = (s32[16]{0:T(128)S(1)}, s32[16]{0:T(128)}, u32[]{:S(2)}) copy-start(s32[16]{0:T(128)} %param.16) | copy-start | bytes 196
  144.7 471.5 %reduce-scatter.3.cloned.1.call-start = ((), (), s32[]{:S(2)}) async-start(), calls=%async_computation.6 | async-start | bytes 12779520 | tf_op jit(solution)/shard_map/reduce_scatter | solution.py:138
  342.4 18.4 %copy-start.5 = (f32[34,512,4]{1,2,0:T(4,128)S(1)}, f32[34,512,4]{1,2,0:T(4,128)}, u32[]{:S(2)}) copy-start(f32[34,512,4]{1,2,0:T(4,128)} %get-tuple-element.7) | copy-start | bytes 835588
  461.6 0.7 copy-start.8
  461.6 155.7 %copy-start.6 = (bf16[256,1024]{1,0:T(8,128)(2,1)S(1)}, bf16[256,1024]{1,0:T(8,128)(2,1)}, u32[]{:S(2)}) copy-start(bf16[256,1024]{1,0:T(8,128)(2,1)} %param.21) | copy-start | bytes 1572868
  461.6 206.6 %copy-start.7 = (f32[1024]{0:T(1024)S(1)}, f32[1024]{0:T(1024)}, u32[]{:S(2)}) copy-start(f32[1024]{0:T(1024)} %param.24) | copy-start | bytes 12292
  461.6 204.8 %all-reduce.5.cloned.1.call-start = ((), (), s32[]{:S(2)}) async-start(), calls=%async_computation.7 | async-start | bytes 524288 | tf_op jit(solution)/shard_map/psum | solution.py:143
  739.7 9.4 %copy-start.3 = (bf16[128,1024]{1,0:T(8,128)(2,1)S(1)}, bf16[128,1024]{1,0:T(8,128)(2,1)}, u32[]{:S(2)}) copy-start(bf16[128,1024]{1,0:T(8,128)(2,1)} %all-reduce.5.cloned.1.call-done) | copy-start | bytes 786436
  741.9 56.7 %all-to-all-start.1 = ((bf16[64,1,10,1024]{3,2,1,0:T(8,128)(2,1)}), bf16[64,1,10,1024]{3,2,1,0:T(8,128)(2,1)S(1)}, u32[]{:S(2)}, u32[]{:S(2)}) async-start(bf16[64,1,10,1024]{3,2,1,0:T(8,128)(2,1)} %copy.146), calls=%async_computation.2 | async-start | bytes 4194304 | tf_op jit(solution)/shard_map/all_to_all | solution.py:178
  748.8 73.0 %reduce-scatter.5.cloned.1.call-start = ((), (), s32[]{:S(2)}) async-start(), calls=%async_computation.8 | async-start | bytes 327680 | tf_op jit(solution)/shard_map/reduce_scatter | solution.py:188
Sparse Core Ops, SparseCore 0:
  10.1 83.1 all-gather.1
  144.9 173.2 all-reduce.2
  461.7 154.4 reduce-scatter.2
  619.3 47.0 all-reduce.4
  803.9 17.9 reduce-scatter.4

commit v2 on v1

--- a/solution.py
+++ b/solution.py
@@ -117,31 +117,66 @@
     probs = jnp.where(mask[:, None], jnp.exp(scores - m_block[..., None]), 0.0)
     l_block = jnp.sum(probs, axis=-1)
     acc_block = jnp.einsum(
-        "bhqk,bkhd->bqhd", probs.astype(jnp.bfloat16), values, preferred_element_type=jnp.float32
+        "bhqk,bkhd->bhqd", probs.astype(jnp.bfloat16), values, preferred_element_type=jnp.float32
     )
     onehot = owners[:, None] == jnp.arange(request_total, dtype=jnp.int32)[None, :]
     m_local = jnp.max(jnp.where(onehot[:, :, None, None], m_block[:, None], NEGATIVE), axis=0)
-    m_global = lax.pmax(m_local, "seq")
-    factor = jnp.exp(m_block - m_global[jnp.maximum(owners, 0)])
-    scaled_acc = acc_block * jnp.transpose(factor, (0, 2, 1))[..., None]
-    scaled_l = jnp.transpose(l_block * factor, (0, 2, 1))
-    packed_state = jnp.concatenate(
-        [scaled_acc.reshape(owners.shape[0], span_rows, -1), scaled_l], axis=2
-    )
-    state_width = packed_state.shape[2]
-    folded_state = jnp.einsum(
-        "br,bx->rx",
-        onehot.astype(jnp.float32),
-        packed_state.reshape(owners.shape[0], -1),
+    factor = jnp.exp(m_block - m_local[jnp.maximum(owners, 0)])
+    weights = onehot.astype(jnp.float32)
+    acc_req = jnp.einsum(
+        "br,bhqd->rhqd",
+        weights,
+        acc_block * factor[..., None],
         precision=lax.Precision.HIGHEST,
-    ).reshape(request_total * span_rows, state_width)
-    own_state = lax.psum_scatter(folded_state, "seq", scatter_dimension=0, tiled=True)
-    acc_fin = own_state[:, : local_heads * DH].reshape(tok_rows, local_heads, DH)
-    l_fin = own_state[:, local_heads * DH :]
-    attention = (acc_fin / l_fin[:, :, None]).reshape(tok_rows, -1).astype(jnp.bfloat16)
-    head_terms = jnp.dot(attention, w_out, preferred_element_type=jnp.float32)
-    mid = hidden.astype(jnp.float32) + lax.psum(head_terms.astype(jnp.bfloat16), "tp").astype(
-        jnp.float32
+    )
+    l_req = jnp.einsum("br,bhq->rhq", weights, l_block * factor, precision=lax.Precision.HIGHEST)
+    quarters = span_rows // tok_rows
+    acc_req = jnp.transpose(
+        acc_req.reshape(request_total, local_heads, quarters, tok_rows, DH), (0, 2, 1, 3, 4)
+    )
+    stats = jnp.stack([m_local, l_req], axis=-1)
+    stats = jnp.transpose(
+        stats.reshape(request_total, local_heads, quarters, tok_rows, 2), (0, 2, 1, 3, 4)
+    )
+    bit_count = seq_count.bit_length() - 1
+    acc_req = acc_req.reshape((2,) * bit_count + acc_req.shape[2:])
+    stats = stats.reshape((2,) * bit_count + stats.shape[2:])
+    remaining = list(range(bit_count - 1, -1, -1))
+    for bit in ([0, 1, 3, 2, 4, 5] if bit_count == 6 else list(range(bit_count))):
+        axis = remaining.index(bit)
+        remaining.pop(axis)
+        own_bit = (seq_index >> bit) & 1
+        keep_acc = lax.dynamic_index_in_dim(acc_req, own_bit, axis, keepdims=False)
+        send_acc = lax.dynamic_index_in_dim(acc_req, 1 - own_bit, axis, keepdims=False)
+        keep_stats = lax.dynamic_index_in_dim(stats, own_bit, axis, keepdims=False)
+        send_stats = lax.dynamic_index_in_dim(stats, 1 - own_bit, axis, keepdims=False)
+        pairs = [(source, source ^ (1 << bit)) for source in range(seq_count)]
+        got_acc = lax.ppermute(send_acc.astype(jnp.bfloat16), "seq", pairs).astype(jnp.float32)
+        got_stats = lax.ppermute(send_stats, "seq", pairs)
+        m_new = jnp.maximum(keep_stats[..., 0], got_stats[..., 0])
+        keep_factor = jnp.exp(keep_stats[..., 0] - m_new)
+        got_factor = jnp.exp(got_stats[..., 0] - m_new)
+        l_new = keep_stats[..., 1] * keep_factor + got_stats[..., 1] * got_factor
+        acc_req = keep_acc * keep_factor[..., None] + got_acc * got_factor[..., None]
+        stats = jnp.stack([m_new, l_new], axis=-1)
+    attention = jnp.transpose(acc_req / stats[..., 1:2], (1, 0, 2)).reshape(tok_rows, -1)
+    attention = attention.astype(jnp.bfloat16)
+    tp_count = lax.axis_size("tp")
+    tp_index = lax.axis_index("tp")
+
+    def tp_gather(value, axis):
+        pieces = [value] + [
+            lax.ppermute(value, "tp", [(i, (i + k) % tp_count) for i in range(tp_count)])
+            for k in range(1, tp_count)
+        ]
+        stacked = jnp.stack(pieces, axis=0)
+        ordered = jnp.take(stacked, (tp_index - jnp.arange(tp_count)) % tp_count, axis=0)
+        return jnp.concatenate([ordered[j] for j in range(tp_count)], axis=axis)
+
+    full_attention = tp_gather(attention, 1)
+    full_w_out = tp_gather(w_out, 0)
+    mid = hidden.astype(jnp.float32) + jnp.dot(
+        full_attention, full_w_out, preferred_element_type=jnp.float32
     )
     moe_in = (rms_rows(mid) * moe_gain).astype(jnp.bfloat16)
     logits = jnp.dot(moe_in.astype(jnp.float32), router, precision=lax.Precision.HIGHEST)

time: 833 us -> 488 us (0.59)
  waiting for transfers between devices: 488 us -> 164 us
  local copies, waits for them, and re-layouts: 142 us -> 87.7 us
  starting transfers between devices: 7.31 us -> 36.5 us
  other arithmetic: 48.6 us -> 37.1 us
  matrix products: 68.6 us -> 77.9 us
    pmax x1 -> x0, waiting for transfers between devices: 156 us -> none  [shards(): m_global = lax.pmax(m_local, 'seq')]
    reduce_scatter x1 -> x0, waiting for transfers between devices: 152 us -> none  [shards(): lax.psum_scatter(folded_state, 'seq', scatter_dimension=0, tiled=True)]
    reshape x3 -> x1, local copies, waits for them, and re-layouts: 79.6 us -> 10.1 us  [shards(): acc_req.reshape(request_total, local_heads, quarters, tok_rows, DH)]
    psum x1 -> x0, waiting for transfers between devices: 47.2 us -> none  [shards(): lax.psum(head_terms.astype(jnp.bfloat16), 'tp').astype(jnp.float32)]
    ppermute x0 -> x18, waiting for transfers between devices: none -> 40.9 us  [the longest x6 36.7 us: shards(): lax.ppermute(send_acc.astype(jnp.bfloat16), 'seq', pairs)]
    ppermute x0 -> x18, starting transfers between devices: none -> 29.4 us  [the longest x6 11.3 us: tp_gather(): lax.ppermute(value, 'tp', [(i, (i + k) % tp_count) for i in range(tp_coun...]
    concatenate x1 -> x0, other arithmetic: 19.7 us -> none  [shards(): jnp.concatenate([scaled_acc.reshape(owners.shape[0], span_rows, -1), scal...]
    dot_general x3 -> x4, matrix products: 36.8 us -> 48.4 us  [the longest x1 25.1 us: shards(): jnp.einsum('br,bhqd->rhqd', weights, acc_block * factor[..., None], preci...]
  transfers between devices with their start and end apart: 6 -> 21, of which waited for: 6 -> 12; matrix products, arithmetic and copies ran while one was open for 5% -> 37% of each run, Pallas kernels for 0% -> 0%
where the time goes in v2:
time: 488 us; the launch traced here: 482 us
  waiting for transfers between devices  164 us (34%)
  local copies, waits for them, and re-layouts  87.7 us (18%)
  matrix products  77.9 us (16%)
  blocking collectives  64.6 us (13%)
  other arithmetic  37.1 us (8%)
  starting transfers between devices  36.5 us (7%)
  between operations  14.3 us (3%)
    all_to_all x1, blocking collectives, shards(): lax.all_to_all(outgoing, 'seq', split_axis=0, concat_axis=0, tiled=True)  64.6 us
    all_gather x1, waiting for transfers between devices, shards(): lax.all_gather(queries, 'seq', axis=0, tiled=True)  58.8 us
    all_to_all x1, waiting for transfers between devices, shards(): lax.all_to_all(produced.astype(jnp.bfloat16), 'seq', split_axis=0, concat...  45.8 us
    ppermute x6, waiting for transfers between devices, shards(): lax.ppermute(send_acc.astype(jnp.bfloat16), 'seq', pairs)  36.7 us
    reshape x2, local copies, waits for them, and re-layouts, shards(): lax.all_gather(queries, 'seq', axis=0, tiled=True)  25.7 us
    dot_general x1, matrix products, shards(): jnp.einsum('br,bhqd->rhqd', weights, acc_block * factor[..., None], preci...  25.1 us
    dot_general x1, matrix products, shards(): jnp.einsum('bhqk,bkhd->bhqd', probs.astype(jnp.bfloat16), values, preferr...  21.5 us
    reduce_scatter x1, waiting for transfers between devices, shards(): lax.psum_scatter(mixture.astype(jnp.bfloat16), 'tp', scatter_dimension=1,...  18.6 us
  transfers between devices with their start and end apart: 21, of which 12 were waited for; matrix products, arithmetic and copies ran while one was open for 37% of the time, Pallas kernels for 0%

profile of v2, /device:TPU:1, one launch (start us, length us, event | category | flops | bytes accessed | tf_op | source)
XLA Modules:
  0.0 482.3 jit_solution(15697876299836480089)
XLA Ops:
  12.0 2.6 collective-permute-start.16
  19.6 2.4 copy.110
  25.9 4.1 copy.112
  34.6 58.8 %all-gather.2.cloned.1.call-done = bf16[8192,256]{1,0:T(8,128)(2,1)} async-done(((bf16[128,256]{1,0:T(8,128)(2,1)}), bf16[8192,256]{1,0:T(8,128)(2,1)}) %all-gather.2.cloned.1.call-update) | async-done | bytes 4194320 | tf_op jit(solution)/shard_map/all_gather | solution.py:108
  93.4 13.0 %reshape.474 = bf16[16,512,4,64]{3,2,1,0:T(4,128)(2,1)} reshape(bf16[8192,256]{1,0:T(8,128)(2,1)} %all-gather.2.cloned.1.call-done) | data formatting | bytes 8388608 | tf_op jit(solution)/shard_map/reshape | solution.py:108
  106.3 12.7 %copy.109 = bf16[16,512,4,64]{1,3,2,0:T(8,128)(2,1)} copy(bf16[16,512,4,64]{3,2,1,0:T(4,128)(2,1)} %reshape.474) | data formatting | bytes 8388608 | tf_op jit(solution)/shard_map/reshape | solution.py:108
  119.1 7.5 %gather_fusion.1 = bf16[34,512,4,64]{1,3,2,0:T(8,128)(2,1)} fusion(bf16[16,512,4,64]{1,3,2,0:T(8,128)(2,1)} %copy.109, s32[1024]{0:T(1024)S(1)} %pad_clamp_fusion.1), kind=kCustom, calls=%fused_computation.1 | custom fusion | bytes 17825928 | tf_op jit(solution)/shard_map/gather | solution.py:111
  126.5 17.1 %fusion = (f32[34,4,512]{2,1,0:T(4,128)S(1)}, f32[34,4,512,128]{2,3,1,0:T(8,128)}) fusion(pred[34,512,128]{1,2,0:T(8,128)(4,1)S(1)} %pad_add_fusion, bf16[34,512,4,64]{1,3,2,0:T(8,128)(2,1)} %gather_fusion.1, bf16[1,128,4,64]{1,3,2,0:T(8,128)(2,1)S(1)} %bitcast.238, bf16[33,128,4,64]{1,3,2,0:T(8,128)(2,1)} %bitcast.223), kind=kOutput, calls=%fused_computation.8 | convolution fusion | flops 1168633856 | bytes 49299456 | tf_op jit(solution)/shard_map/bqhd,bkhd->bhqk/dot_general | solution.py:112
  143.6 17.5 %fusion.1 = f32[34,4,512]{2,1,0:T(4,128)} fusion(f32[34,4,512,128]{2,3,1,0:T(8,128)} %get-tuple-element.56, f32[34,4,512]{2,1,0:T(4,128)S(1)} %get-tuple-element.55, pred[34,512,128]{1,2,0:T(8,128)(4,1)S(1)} %pad_add_fusion), kind=kLoop, calls=%fused_computation.9 | loop fusion | flops 44494848 | bytes 38436864 | tf_op jit(solution)/shard_map/reduce_sum | solution.py:118
  163.0 2.5 gather_fusion.2
  167.3 21.5 %broadcast_multiply_fusion = f32[34,4,512,64]{2,3,1,0:T(8,128)} fusion(f32[34,4,512]{2,1,0:T(4,128)S(1)} %bitcast.232, f32[34,4,512,128]{2,3,1,0:T(8,128)} %get-tuple-element.56, f32[34,4,512]{2,1,0:T(4,128)S(1)} %get-tuple-element.55, pred[34,512,128]{1,2,0:T(8,128)(4,1)S(1)} %pad_add_fusion, bf16[1,128,4,64]{1,3,2,0:T(8,128)(2,1)S(1)} %bitcast.239, ...), kind=kOutput, calls=%fused_computation.19 | convolution fusion | flops 1194328064 | bytes 58490880 | tf_op jit(solution)/shard_map/bhqk,bkhd->bhqd/dot_general | solution.py:119
  188.7 25.1 %fusion.3 = f32[16,4,512,64]{2,0,3,1:T(8,128)} fusion(f32[34,4,512,64]{2,3,1,0:T(8,128)} %broadcast_multiply_fusion, s32[34]{0:T(128)S(1)} %copy-done.18), kind=kOutput, calls=%fused_computation.11 | convolution fusion | flops 855638528 | bytes 26214536 | tf_op jit(solution)/shard_map/br,bhqd->rhqd/dot_general | solution.py:126
  213.8 10.1 %reshape.409 = f32[16,4,4,128,64]{3,2,0,4,1:T(4,128)} reshape(f32[16,4,512,64]{2,0,3,1:T(8,128)} %fusion.3) | data formatting | bytes 16777216 | tf_op jit(solution)/shard_map/reshape | solution.py:135
  223.9 8.2 %copy.118 = f32[16,4,4,128,64]{3,4,2,1,0:T(8,128)S(1)} copy(f32[16,4,4,128,64]{3,1,0,4,2:T(4,128)} %bitcast.217) | data formatting | bytes 16777216 | tf_op jit(solution)/shard_map/transpose | solution.py:134
  232.2 3.2 copy-done.2
  237.7 2.9 pad_maximum_fusion
  240.6 2.3 gather_fusion.4
  247.1 4.0 fusion.14
  253.5 2.5 collective-permute-done.4
  257.9 17.8 %collective-permute-done.3 = bf16[2,2,2,2,4,128,64]{5,6,4,3,2,1,0:T(8,128)(2,1)S(1)} collective-permute-done((bf16[2,2,2,2,4,128,64]{5,6,4,3,2,1,0:T(8,128)(2,1)S(1)}, bf16[2,2,2,2,4,128,64]{5,6,4,3,2,1,0:T(8,128)(2,1)S(1)}, u32[]{:S(2)}, u32[]{:S(2)}) %collective-permute-start.3) | collective-permute-done | bytes 1048608 | tf_op jit(solution)/shard_map/ppermute | solution.py:154
  277.0 2.3 collective-permute-start.8
  279.3 9.4 %collective-permute-done.5 = bf16[2,2,2,4,128,64]{4,5,3,2,1,0:T(8,128)(2,1)S(1)} collective-permute-done((bf16[2,2,2,4,128,64]{4,5,3,2,1,0:T(8,128)(2,1)S(1)}, bf16[2,2,2,4,128,64]{4,5,3,2,1,0:T(8,128)(2,1)S(1)}, u32[]{:S(2)}, u32[]{:S(2)}) %collective-permute-start.5) | collective-permute-done | bytes 524320 | tf_op jit(solution)/shard_map/ppermute | solution.py:154
  291.1 3.1 collective-permute-start.10
  298.6 3.7 collective-permute-done.9
  302.4 3.4 collective-permute-start.11
  305.7 3.7 collective-permute-done.11
  310.8 2.5 collective-permute-start.13
  320.4 64.6 %all_to_all.10 = bf16[64,1,10,1024]{3,2,1,0:T(8,128)(2,1)S(1)} all-to-all(bf16[64,1,10,1024]{3,2,1,0:T(8,128)(2,1)S(1)} %bitcast.221), channel_id=1, replica_groups=mesh['seq'=64,'tp'=4] {'seq'}, dimensions={0} | all-to-all | bytes 2621440 | tf_op jit(solution)/shard_map/all_to_all | solution.py:201
  386.3 2.4 fusion.48
  393.1 7.1 %all-to-all-start.1 = ((bf16[64,1,10,1024]{3,2,1,0:T(8,128)(2,1)}), bf16[64,1,10,1024]{3,2,1,0:T(8,128)(2,1)S(1)}, u32[]{:S(2)}, u32[]{:S(2)}) async-start(bf16[64,1,10,1024]{3,2,1,0:T(8,128)(2,1)} %copy.130), calls=%async_computation.1 | async-start | bytes 4194304 | tf_op jit(solution)/shard_map/all_to_all | solution.py:213
  404.1 45.8 %all-to-all-done.1 = bf16[64,1,10,1024]{3,2,1,0:T(8,128)(2,1)S(1)} async-done(((bf16[64,1,10,1024]{3,2,1,0:T(8,128)(2,1)}), bf16[64,1,10,1024]{3,2,1,0:T(8,128)(2,1)S(1)}, u32[]{:S(2)}, u32[]{:S(2)}) %all-to-all-start.1) | async-done | bytes 1310752 | tf_op jit(solution)/shard_map/all_to_all | solution.py:213
  455.2 18.6 %reduce-scatter.2.cloned.1.call-done = bf16[128,256]{1,0:T(8,128)(2,1)} async-done(((bf16[128,1024]{1,0:T(8,128)(2,1)}), bf16[128,256]{1,0:T(8,128)(2,1)}) %reduce-scatter.2.cloned.1.call-update) | async-done | bytes 65552 | tf_op jit(solution)/shard_map/reduce_scatter | solution.py:223
  (185 shorter events, 65.6 us)
Async XLA Ops:
  6.5 383.5 %copy-start = (bf16[1,352,1024]{2,1,0:T(8,128)(2,1)S(1)}, bf16[1,352,1024]{2,1,0:T(8,128)(2,1)}, u32[]{:S(2)}) copy-start(bf16[1,352,1024]{2,1,0:T(8,128)(2,1)} %param.27) | copy-start | bytes 2162692
  6.5 13.0 %copy-start.6 = (bf16[33,128,256]{2,1,0:T(8,128)(2,1)S(1)}, bf16[33,128,256]{2,1,0:T(8,128)(2,1)}, u32[]{:S(2)}) copy-start(bf16[33,128,256]{2,1,0:T(8,128)(2,1)} %param.22) | copy-start | bytes 6488068
  6.5 86.8 %all-gather.2.cloned.1.call-start = ((), (), s32[]{:S(2)}) async-start(), calls=%async_computation.3 | async-start | bytes 4259840 | tf_op jit(solution)/shard_map/all_gather | solution.py:108
  9.8 227.8 %collective-permute-start.15 = (bf16[256,1024]{1,0:T(8,128)(2,1)}, bf16[256,1024]{1,0:T(8,128)(2,1)}, u32[]{:S(2)}, u32[]{:S(2)}) collective-permute-start(bf16[256,1024]{1,0:T(8,128)(2,1)} %param.21), channel_id=1, source_target_pairs={{0,1},{1,2},{2,3},{3,0},{4,5},{5,6},{6,7},{7,4},{8,9},{9,10},{10,1... | collective-permute-start | bytes 1572872 | tf_op jit(solution)/shard_map/ppermute | solution.py:169
  12.0 225.6 %collective-permute-start.16 = (bf16[256,1024]{1,0:T(8,128)(2,1)}, bf16[256,1024]{1,0:T(8,128)(2,1)}, u32[]{:S(2)}, u32[]{:S(2)}) collective-permute-start(bf16[256,1024]{1,0:T(8,128)(2,1)} %param.21), channel_id=1, source_target_pairs={{0,2},{1,3},{2,0},{3,1},{4,6},{5,7},{6,4},{7,5},{8,10},{9,11},{10,... | collective-permute-start | bytes 1572872 | tf_op jit(solution)/shard_map/ppermute | solution.py:169
  14.7 223.0 %collective-permute-start.17 = (bf16[256,1024]{1,0:T(8,128)(2,1)}, bf16[256,1024]{1,0:T(8,128)(2,1)}, u32[]{:S(2)}, u32[]{:S(2)}) collective-permute-start(bf16[256,1024]{1,0:T(8,128)(2,1)} %param.21), channel_id=1, source_target_pairs={{0,3},{1,0},{2,1},{3,2},{4,7},{5,4},{6,5},{7,6},{8,11},{9,8},{10,9... | collective-permute-start | bytes 1572872 | tf_op jit(solution)/shard_map/ppermute | solution.py:169
  23.2 6.9 %copy-start.17 = (s32[34]{0:T(128)}, s32[34]{0:T(128)S(1)}, u32[]{:S(2)}) copy-start(s32[34]{0:T(128)S(1)} %pad_add_fusion.1) | copy-start | bytes 412
  32.4 86.7 %copy-start.16 = (s32[1024]{0:T(1024)}, s32[1024]{0:T(1024)S(1)}, u32[]{:S(2)}) copy-start(s32[1024]{0:T(1024)S(1)} %pad_clamp_fusion.1) | copy-start | bytes 12292
  143.6 17.5 %copy-start.13 = (pred[34,16]{1,0:T(8,128)(4,1)S(1)}, pred[34,16]{1,0:T(8,128)(4,1)}, u32[]{:S(2)}) copy-start(pred[34,16]{1,0:T(8,128)(4,1)} %copy.115) | copy-start | bytes 1636
  161.1 6.1 %copy-start.12 = (bf16[128,256]{0,1:T(8,128)(2,1)S(1)}, bf16[128,256]{0,1:T(8,128)(2,1)}, u32[]{:S(2)}) copy-start(bf16[128,256]{0,1:T(8,128)(2,1)} %copy.113) | copy-start | bytes 196612
  167.3 21.5 %copy-start.18 = (s32[34]{0:T(128)S(1)}, s32[34]{0:T(128)}, u32[]{:S(2)}) copy-start(s32[34]{0:T(128)} %copy-done.17) | copy-start | bytes 412
  232.2 5.4 %copy-start.15 = (s32[128,2]{0,1:T(2,128)S(1)}, s32[128,2]{0,1:T(2,128)}, u32[]{:S(2)}) copy-start(s32[128,2]{0,1:T(2,128)} %param.17) | copy-start | bytes 3076
  232.2 5.4 %copy-start.20 = (s32[128,2]{0,1:T(2,128)S(1)}, s32[128,2]{0,1:T(2,128)}, u32[]{:S(2)}) copy-start(s32[128,2]{0,1:T(2,128)} %copy.125) | copy-start | bytes 3076
  232.2 5.5 %copy-start.11 = (bf16[256,1024]{1,0:T(8,128)(2,1)S(1)}, bf16[256,1024]{1,0:T(8,128)(2,1)}, u32[]{:S(2)}) copy-start(bf16[256,1024]{1,0:T(8,128)(2,1)} %param.21) | copy-start | bytes 1572868
  237.3 9.8 %collective-permute-start.1 = (bf16[2,2,2,2,2,4,128,64]{6,7,5,4,3,2,1,0:T(8,128)(2,1)}, bf16[2,2,2,2,2,4,128,64]{6,7,5,4,3,2,1,0:T(8,128)(2,1)}, u32[]{:S(2)}, u32[]{:S(2)}) collective-permute-start(bf16[2,2,2,2,2,4,128,64]{6,7,5,4,3,2,1,0:T(8,128)(2,1)} %fusion.22), channel_id=1, source_target_pairs={{0,4},{4,0},{8,12},{12,8},{16,20},{20,16},{24,28},{28,24},{32,36},... | collective-permute-start | bytes 6291464 | tf_op jit(solution)/shard_map/ppermute | solution.py:154
  245.4 1.4 collective-permute-start
  246.9 5.9 %collective-permute-start.2 = (f32[2,2,2,2,4,128,2]{5,4,3,2,1,0,6:T(4,128)S(1)}, f32[2,2,2,2,4,128,2]{5,4,3,2,1,0,6:T(4,128)S(1)}, u32[]{:S(2)}, u32[]{:S(2)}) collective-permute-start(f32[2,2,2,2,4,128,2]{5,4,3,2,1,0,6:T(4,128)S(1)} %get-tuple-element.30), channel_id=1, source_target_pairs={{0,8},{4,12},{8,0},{12,4},{16,24},{20,28},{24,16},{28,20},{32,40},... | collective-permute-start | bytes 196616 | tf_op jit(solution)/shard_map/ppermute | solution.py:155
  251.3 24.4 %collective-permute-start.3 = (bf16[2,2,2,2,4,128,64]{5,6,4,3,2,1,0:T(8,128)(2,1)S(1)}, bf16[2,2,2,2,4,128,64]{5,6,4,3,2,1,0:T(8,128)(2,1)S(1)}, u32[]{:S(2)}, u32[]{:S(2)}) collective-permute-start(bf16[2,2,2,2,4,128,64]{5,6,4,3,2,1,0:T(8,128)(2,1)S(1)} %fusion.37), channel_id=1, source_target_pairs={{0,8},{4,12},{8,0},{12,4},{16,24},{20,28},{24,16},{28,20},{32,40},... | collective-permute-start | bytes 3145736 | tf_op jit(solution)/shard_map/ppermute | solution.py:154
  252.9 3.1 collective-permute-start.4
  256.1 20.9 %collective-permute-start.6 = (f32[2,2,4,128,2]{3,2,1,0,4:T(4,128)S(1)}, f32[2,2,4,128,2]{3,2,1,0,4:T(4,128)S(1)}, u32[]{:S(2)}, u32[]{:S(2)}) collective-permute-start(f32[2,2,4,128,2]{3,2,1,0,4:T(4,128)S(1)} %get-tuple-element.36), channel_id=1, source_target_pairs={{0,16},{4,20},{8,24},{12,28},{16,0},{20,4},{24,8},{28,12},{32,48},... | collective-permute-start | bytes 49160 | tf_op jit(solution)/shard_map/ppermute | solution.py:155
  276.4 12.4 %collective-permute-start.5 = (bf16[2,2,2,4,128,64]{4,5,3,2,1,0:T(8,128)(2,1)S(1)}, bf16[2,2,2,4,128,64]{4,5,3,2,1,0:T(8,128)(2,1)S(1)}, u32[]{:S(2)}, u32[]{:S(2)}) collective-permute-start(bf16[2,2,2,4,128,64]{4,5,3,2,1,0:T(8,128)(2,1)S(1)} %fusion.54), channel_id=1, source_target_pairs={{0,32},{4,36},{8,40},{12,44},{16,48},{20,52},{24,56},{28,60},{32,0... | collective-permute-start | bytes 1572872 | tf_op jit(solution)/shard_map/ppermute | solution.py:154
  277.0 14.0 %collective-permute-start.8 = (f32[2,4,128,2]{2,1,0,3:T(4,128)S(1)}, f32[2,4,128,2]{2,1,0,3:T(4,128)S(1)}, u32[]{:S(2)}, u32[]{:S(2)}) collective-permute-start(f32[2,4,128,2]{2,1,0,3:T(4,128)S(1)} %get-tuple-element.40), channel_id=1, source_target_pairs={{0,64},{4,68},{8,72},{12,76},{16,80},{20,84},{24,88},{28,92},{32,9... | collective-permute-start | bytes 24584 | tf_op jit(solution)/shard_map/ppermute | solution.py:155
  289.1 7.2 %collective-permute-start.7 = (bf16[2,2,4,128,64]{3,4,2,1,0:T(8,128)(2,1)S(1)}, bf16[2,2,4,128,64]{3,4,2,1,0:T(8,128)(2,1)S(1)}, u32[]{:S(2)}, u32[]{:S(2)}) collective-permute-start(bf16[2,2,4,128,64]{3,4,2,1,0:T(8,128)(2,1)S(1)} %fusion.60), channel_id=1, source_target_pairs={{0,16},{4,20},{8,24},{12,28},{16,0},{20,4},{24,8},{28,12},{32,48},... | collective-permute-start | bytes 786440 | tf_op jit(solution)/shard_map/ppermute | solution.py:154
  291.1 14.6 %collective-permute-start.10 = (f32[4,128,2]{1,0,2:T(4,128)S(1)}, f32[4,128,2]{1,0,2:T(4,128)S(1)}, u32[]{:S(2)}, u32[]{:S(2)}) collective-permute-start(f32[4,128,2]{1,0,2:T(4,128)S(1)} %get-tuple-element.47), channel_id=1, source_target_pairs={{0,128},{4,132},{8,136},{12,140},{16,144},{20,148},{24,152},{28,15... | collective-permute-start | bytes 12296 | tf_op jit(solution)/shard_map/ppermute | solution.py:155
  296.5 5.8 %collective-permute-start.9 = (bf16[2,4,128,64]{2,3,1,0:T(8,128)(2,1)S(1)}, bf16[2,4,128,64]{2,3,1,0:T(8,128)(2,1)S(1)}, u32[]{:S(2)}, u32[]{:S(2)}) collective-permute-start(bf16[2,4,128,64]{2,3,1,0:T(8,128)(2,1)S(1)} %fusion.69), channel_id=1, source_target_pairs={{0,64},{4,68},{8,72},{12,76},{16,80},{20,84},{24,88},{28,92},{32,9... | collective-permute-start | bytes 393224 | tf_op jit(solution)/shard_map/ppermute | solution.py:154
  302.4 7.1 %collective-permute-start.11 = (bf16[4,128,64]{1,2,0:T(8,128)(2,1)S(1)}, bf16[4,128,64]{1,2,0:T(8,128)(2,1)S(1)}, u32[]{:S(2)}, u32[]{:S(2)}) collective-permute-start(bf16[4,128,64]{1,2,0:T(8,128)(2,1)S(1)} %fusion.73), channel_id=1, source_target_pairs={{0,128},{4,132},{8,136},{12,140},{16,144},{20,148},{24,152},{28,15... | collective-permute-start | bytes 196616 | tf_op jit(solution)/shard_map/ppermute | solution.py:154
  309.5 5.9 %collective-permute-start.12 = (bf16[128,256]{0,1:T(8,128)(2,1)S(1)}, bf16[128,256]{0,1:T(8,128)(2,1)S(1)}, u32[]{:S(2)}, u32[]{:S(2)}) collective-permute-start(bf16[128,256]{0,1:T(8,128)(2,1)S(1)} %bitcast.233), channel_id=1, source_target_pairs={{0,1},{1,2},{2,3},{3,0},{4,5},{5,6},{6,7},{7,4},{8,9},{9,10},{10,1... | collective-permute-start | bytes 196616 | tf_op jit(solution)/shard_map/ppermute | solution.py:169
  310.8 4.8 collective-permute-start.13
  313.2 3.1 collective-permute-start.14
  393.1 7.4 %copy-start.5 = (f32[128,1024]{1,0:T(8,128)S(1)}, f32[128,1024]{1,0:T(8,128)}, u32[]{:S(2)}) copy-start(f32[128,1024]{1,0:T(8,128)} %copy-done.4) | copy-start | bytes 1572868
  393.1 56.8 %all-to-all-start.1 = ((bf16[64,1,10,1024]{3,2,1,0:T(8,128)(2,1)}), bf16[64,1,10,1024]{3,2,1,0:T(8,128)(2,1)S(1)}, u32[]{:S(2)}, u32[]{:S(2)}) async-start(bf16[64,1,10,1024]{3,2,1,0:T(8,128)(2,1)} %copy.130), calls=%async_computation.1 | async-start | bytes 4194304 | tf_op jit(solution)/shard_map/all_to_all | solution.py:213
  400.2 73.6 %reduce-scatter.2.cloned.1.call-start = ((), (), s32[]{:S(2)}) async-start(), calls=%async_computation.4 | async-start | bytes 327680 | tf_op jit(solution)/shard_map/reduce_scatter | solution.py:223
  (12 other events, 33.0 us)
Sparse Core Ops, SparseCore 0:
  10.1 83.2 all-gather.1
  455.3 18.4 reduce-scatter.1

commit v3 on v2

--- a/solution.py
+++ b/solution.py
@@ -2,6 +2,8 @@
 import jax.numpy as jnp
 from jax import lax
 from jax.sharding import PartitionSpec as P
+from jax.experimental import pallas as pl
+from jax.experimental.pallas import tpu as pltpu
 
 DH = 64
 EXPERTS = 32
@@ -38,6 +40,82 @@
         "hnk,khd->nhd", probs.astype(jnp.bfloat16), values, preferred_element_type=jnp.float32
     )
     return (m_new, l_new, accum * factor[:, :, None] + weighted)
+
+
+def attend_kernel(
+    own_ref, page_ref, limit_ref, offset_ref, fresh_ref,
+    q_ref, k_ref, v_ref, nk_ref, nv_ref, acc_ref, m_ref, l_ref,
+):
+    step = pl.program_id(0)
+    owner = own_ref[step]
+    first = (step == 0) | (own_ref[jnp.maximum(step - 1, 0)] != owner)
+
+    @pl.when(first)
+    def _():
+        acc_ref[...] = jnp.zeros(acc_ref.shape, acc_ref.dtype)
+        m_ref[...] = jnp.full(m_ref.shape, NEGATIVE, m_ref.dtype)
+        l_ref[...] = jnp.zeros(l_ref.shape, l_ref.dtype)
+
+    is_fresh = fresh_ref[step] == 1
+    keys = jnp.where(is_fresh, nk_ref[0], k_ref[0])
+    vals = jnp.where(is_fresh, nv_ref[0], v_ref[0])
+    rows, cols = q_ref.shape[1], keys.shape[0]
+    q_pos = lax.broadcasted_iota(jnp.int32, (rows, cols), 0)
+    k_pos = lax.broadcasted_iota(jnp.int32, (rows, cols), 1)
+    valid = (k_pos < limit_ref[step]) & (q_pos >= offset_ref[step] + k_pos)
+    for h in range(m_ref.shape[1]):
+        lanes = slice(h * DH, (h + 1) * DH)
+        s = lax.dot_general(
+            q_ref[0, :, lanes], keys[:, lanes], (((1,), (1,)), ((), ())),
+            preferred_element_type=jnp.float32,
+        ) * (DH ** (-0.5))
+        s = jnp.where(valid, s, NEGATIVE)
+        m_prev = m_ref[0, h]
+        m_cur = jnp.maximum(m_prev, jnp.max(s, axis=1, keepdims=True))
+        p = jnp.where(valid, jnp.exp(s - m_cur), 0.0)
+        alpha = jnp.exp(m_prev - m_cur)
+        l_ref[0, h] = alpha * l_ref[0, h] + jnp.sum(p, axis=1, keepdims=True)
+        pv = jnp.dot(p.astype(jnp.bfloat16), vals[:, lanes], preferred_element_type=jnp.float32)
+        acc_ref[0, :, lanes] = alpha * acc_ref[0, :, lanes] + pv
+        m_ref[0, h] = m_cur
+
+
+def local_attention(
+    owner, page, limit, offset, fresh, everyone, cache_k, cache_v, new_k, new_v, heads, requests
+):
+    span_rows, width = everyone.shape[1], everyone.shape[2]
+    page_rows = cache_k.shape[1]
+    blocks = owner.shape[0]
+    by_owner = lambda b, own, pg, lim, off, fr: (own[b], 0, 0)
+    by_page = lambda b, own, pg, lim, off, fr: (pg[b], 0, 0)
+    fixed = lambda b, own, pg, lim, off, fr: (0, 0, 0)
+    stat_map = lambda b, own, pg, lim, off, fr: (own[b], 0, 0, 0)
+    grid_spec = pltpu.PrefetchScalarGridSpec(
+        num_scalar_prefetch=5,
+        grid=(blocks,),
+        in_specs=[
+            pl.BlockSpec((1, span_rows, width), by_owner),
+            pl.BlockSpec((1, page_rows, width), by_page),
+            pl.BlockSpec((1, page_rows, width), by_page),
+            pl.BlockSpec((1, page_rows, width), fixed),
+            pl.BlockSpec((1, page_rows, width), fixed),
+        ],
+        out_specs=[
+            pl.BlockSpec((1, span_rows, width), by_owner),
+            pl.BlockSpec((1, heads, span_rows, 1), stat_map),
+            pl.BlockSpec((1, heads, span_rows, 1), stat_map),
+        ],
+    )
+    return pl.pallas_call(
+        attend_kernel,
+        grid_spec=grid_spec,
+        out_shape=[
+            jax.ShapeDtypeStruct((requests, span_rows, width), jnp.float32),
+            jax.ShapeDtypeStruct((requests, heads, span_rows, 1), jnp.float32),
+            jax.ShapeDtypeStruct((requests, heads, span_rows, 1), jnp.float32),
+        ],
+        compiler_params=pltpu.CompilerParams(dimension_semantics=("arbitrary",)),
+    )(owner, page, limit, offset, fresh, everyone, cache_k, cache_v, new_k, new_v)
 
 
 def shards(
@@ -89,57 +167,51 @@
     page_valid = (found >= 0)[:, None] & (
         page_order[:, None] * PAGE + slot_range[None, :] < page_limit[:, None]
     )
-    span_positions = jnp.arange(span_rows, dtype=jnp.int32)
-    fresh_mask = span_positions[:, None] >= own_offset + jnp.arange(tok_rows, dtype=jnp.int32)[None, :]
-    mask = jnp.concatenate(
-        [
-            jnp.broadcast_to(page_valid[:, None, :], (page_count, span_rows, PAGE)),
-            fresh_mask[None],
-        ],
-        axis=0,
-    )
-    owners = jnp.concatenate([page_owner, own_request[None]], axis=0)
-    keys = jnp.concatenate(
-        [cache_k.reshape(page_count, PAGE, local_heads, DH), new_keys[None]], axis=0
-    )
-    values = jnp.concatenate(
-        [cache_v.reshape(page_count, PAGE, local_heads, DH), new_values[None]], axis=0
-    )
+    block_total = page_count + 1
+    owners = jnp.concatenate([jnp.maximum(page_owner, 0), own_request[None]], axis=0)
+    key_limits = jnp.concatenate(
+        [jnp.clip(page_limit - page_order * PAGE, 0, PAGE), jnp.full((1,), PAGE, jnp.int32)], axis=0
+    )
+    query_offsets = jnp.concatenate(
+        [jnp.full((page_count,), -span_rows - PAGE, jnp.int32), own_offset[None]], axis=0
+    )
+    block_order = jnp.argsort(owners, stable=True).astype(jnp.int32)
+    sorted_owner = owners[block_order]
+    sorted_limit = key_limits[block_order]
+    sorted_offset = query_offsets[block_order]
+    sorted_fresh = (block_order == page_count).astype(jnp.int32)
+    sorted_page = jnp.minimum(block_order, page_count - 1)
     everyone = lax.all_gather(queries, "seq", axis=0, tiled=True).reshape(
-        request_total, span_rows, local_heads, DH
-    )
-    rows = everyone[jnp.maximum(owners, 0)]
-    scores = jnp.einsum("bqhd,bkhd->bhqk", rows, keys, preferred_element_type=jnp.float32) * (
-        DH ** (-0.5)
-    )
-    scores = jnp.where(mask[:, None], scores, NEGATIVE)
-    m_block = jnp.max(scores, axis=-1)
-    probs = jnp.where(mask[:, None], jnp.exp(scores - m_block[..., None]), 0.0)
-    l_block = jnp.sum(probs, axis=-1)
-    acc_block = jnp.einsum(
-        "bhqk,bkhd->bhqd", probs.astype(jnp.bfloat16), values, preferred_element_type=jnp.float32
-    )
-    onehot = owners[:, None] == jnp.arange(request_total, dtype=jnp.int32)[None, :]
-    m_local = jnp.max(jnp.where(onehot[:, :, None, None], m_block[:, None], NEGATIVE), axis=0)
-    factor = jnp.exp(m_block - m_local[jnp.maximum(owners, 0)])
-    weights = onehot.astype(jnp.float32)
-    acc_req = jnp.einsum(
-        "br,bhqd->rhqd",
-        weights,
-        acc_block * factor[..., None],
-        precision=lax.Precision.HIGHEST,
-    )
-    l_req = jnp.einsum("br,bhq->rhq", weights, l_block * factor, precision=lax.Precision.HIGHEST)
+        request_total, span_rows, local_heads * DH
+    )
+    width_heads = local_heads * DH
+    acc_out, m_out, l_out = local_attention(
+        sorted_owner,
+        sorted_page,
+        sorted_limit,
+        sorted_offset,
+        sorted_fresh,
+        everyone,
+        cache_k,
+        cache_v,
+        new_keys.reshape(1, tok_rows, width_heads),
+        new_values.reshape(1, tok_rows, width_heads),
+        local_heads,
+        request_total,
+    )
+    visited = jnp.any(
+        sorted_owner[:, None] == jnp.arange(request_total, dtype=jnp.int32)[None, :], axis=0
+    )
+    acc_req = jnp.where(visited[:, None, None], acc_out, 0.0)
+    m_req = jnp.where(visited[:, None, None, None], m_out, NEGATIVE)
+    l_req = jnp.where(visited[:, None, None, None], l_out, 0.0)
     quarters = span_rows // tok_rows
-    acc_req = jnp.transpose(
-        acc_req.reshape(request_total, local_heads, quarters, tok_rows, DH), (0, 2, 1, 3, 4)
-    )
-    stats = jnp.stack([m_local, l_req], axis=-1)
+    stats = jnp.stack([m_req[..., 0], l_req[..., 0]], axis=-1)
     stats = jnp.transpose(
-        stats.reshape(request_total, local_heads, quarters, tok_rows, 2), (0, 2, 1, 3, 4)
+        stats.reshape(request_total, local_heads, quarters, tok_rows, 2), (0, 2, 3, 1, 4)
     )
     bit_count = seq_count.bit_length() - 1
-    acc_req = acc_req.reshape((2,) * bit_count + acc_req.shape[2:])
+    acc_req = acc_req.reshape((2,) * bit_count + (tok_rows, width_heads))
     stats = stats.reshape((2,) * bit_count + stats.shape[2:])
     remaining = list(range(bit_count - 1, -1, -1))
     for bit in ([0, 1, 3, 2, 4, 5] if bit_count == 6 else list(range(bit_count))):
@@ -157,9 +229,15 @@
         keep_factor = jnp.exp(keep_stats[..., 0] - m_new)
         got_factor = jnp.exp(got_stats[..., 0] - m_new)
         l_new = keep_stats[..., 1] * keep_factor + got_stats[..., 1] * got_factor
-        acc_req = keep_acc * keep_factor[..., None] + got_acc * got_factor[..., None]
+        split_shape = keep_acc.shape[:-1] + (local_heads, DH)
+        acc_req = (
+            keep_acc.reshape(split_shape) * keep_factor[..., None]
+            + got_acc.reshape(split_shape) * got_factor[..., None]
+        ).reshape(keep_acc.shape)
         stats = jnp.stack([m_new, l_new], axis=-1)
-    attention = jnp.transpose(acc_req / stats[..., 1:2], (1, 0, 2)).reshape(tok_rows, -1)
+    attention = (
+        acc_req.reshape(tok_rows, local_heads, DH) / stats[..., 1][..., None]
+    ).reshape(tok_rows, -1)
     attention = attention.astype(jnp.bfloat16)
     tp_count = lax.axis_size("tp")
     tp_index = lax.axis_index("tp")

time: 488 us -> 498 us (1.020)
  Pallas kernels: 0 us -> 101 us
  matrix products: 77.9 us -> 13 us
  local copies, waits for them, and re-layouts: 87.7 us -> 61.1 us
  other arithmetic: 37.1 us -> 43.7 us
  waiting for transfers between devices: 164 us -> 170 us
  starting transfers between devices: 36.5 us -> 30.7 us
    pallas_call x0 -> x1, Pallas kernels: none -> 101 us  [local_attention(): pl.pallas_call(attend_kernel, grid_spec=grid_spec, out_shape=[jax.ShapeDt...]
    dot_general x4 -> x0, matrix products: 63.9 us -> none  [the longest x1 25.1 us: shards(): jnp.einsum('br,bhqd->rhqd', weights, acc_block * factor[..., None], preci...]
    reshape x3 -> x1, local copies, waits for them, and re-layouts: 35.8 us -> 1.03 us  [shards(): stats.reshape(request_total, local_heads, quarters, tok_rows, 2)]
    select_n x0 -> x2, other arithmetic: none -> 25.3 us  [the longest x1 21.1 us: shards(): m_req = jnp.where(visited[:, None, None, None], m_out, NEGATIVE)]
    select_n x0 -> x2, local copies, waits for them, and re-layouts: none -> 19.9 us  [the longest x1 9.97 us: shards(): l_req = jnp.where(visited[:, None, None, None], l_out, 0.0)]
    reduce_sum x1 -> x0, other arithmetic: 17.5 us -> none  [shards(): l_block = jnp.sum(probs, axis=-1)]
    dynamic_slice x1 -> x3, local copies, waits for them, and re-layouts: 0.09 us -> 11.5 us  [the longest x2 9.88 us: shards(): keep_acc = lax.dynamic_index_in_dim(acc_req, own_bit, axis, keepdims=False)]
    all_gather x1, waiting for transfers between devices: 58.8 us -> 50.1 us  [shards(): lax.all_gather(queries, 'seq', axis=0, tiled=True)]
  transfers between devices with their start and end apart: 21 -> 21, of which waited for: 12 -> 11; matrix products, arithmetic and copies ran while one was open for 37% -> 17% of each run, Pallas kernels for 0% -> 0%
where the time goes in v3:
time: 498 us; the launch traced here: 496 us
  waiting for transfers between devices  170 us (34%)
  Pallas kernels  101 us (20%)
  blocking collectives  62.8 us (13%)
  local copies, waits for them, and re-layouts  61.1 us (12%)
  other arithmetic  43.7 us (9%)
  starting transfers between devices  30.7 us (6%)
  between operations  14 us (3%)
  matrix products  13 us (3%)
    pallas_call x1, Pallas kernels, local_attention(): pl.pallas_call(attend_kernel, grid_spec=grid_spec, out_shape=[jax.ShapeDt...  101 us
    all_to_all x1, blocking collectives, shards(): lax.all_to_all(outgoing, 'seq', split_axis=0, concat_axis=0, tiled=True)  62.8 us
    all_gather x1, waiting for transfers between devices, shards(): lax.all_gather(queries, 'seq', axis=0, tiled=True)  50.1 us
    all_to_all x1, waiting for transfers between devices, shards(): lax.all_to_all(produced.astype(jnp.bfloat16), 'seq', split_axis=0, concat...  45.8 us
    ppermute x6, waiting for transfers between devices, shards(): lax.ppermute(send_acc.astype(jnp.bfloat16), 'seq', pairs)  43.8 us
    select_n x1, other arithmetic, shards(): m_req = jnp.where(visited[:, None, None, None], m_out, NEGATIVE)  21.1 us
    reduce_scatter x1, waiting for transfers between devices, shards(): lax.psum_scatter(mixture.astype(jnp.bfloat16), 'tp', scatter_dimension=1,...  18.5 us
    ppermute x6, starting transfers between devices, tp_gather(): lax.ppermute(value, 'tp', [(i, (i + k) % tp_count) for i in range(tp_coun...  10.8 us
  transfers between devices with their start and end apart: 21, of which 11 were waited for; matrix products, arithmetic and copies ran while one was open for 17% of the time, Pallas kernels for 0%

profile of v3, /device:TPU:1, one launch (start us, length us, event | category | flops | bytes accessed | tf_op | source)
XLA Modules:
  0.0 496.0 jit_solution(4785351255700611434)
XLA Ops:
  7.8 2.0 convolution_convert_fusion.5
  9.8 2.2 collective-permute-start.15
  12.0 2.6 collective-permute-start.16
  19.4 2.0 sort.17
  29.2 8.3 %collective-permute-done.16 = bf16[256,1024]{1,0:T(8,128)(2,1)} collective-permute-done((bf16[256,1024]{1,0:T(8,128)(2,1)}, bf16[256,1024]{1,0:T(8,128)(2,1)}, u32[]{:S(2)}, u32[]{:S(2)}) %collective-permute-start.16) | collective-permute-done | bytes 524320 | tf_op jit(solution)/shard_map/ppermute | solution.py:247
  43.2 50.1 %all-gather.2.cloned.1.call-done = bf16[8192,256]{1,0:T(8,128)(2,1)} async-done(((bf16[128,256]{1,0:T(8,128)(2,1)}), bf16[8192,256]{1,0:T(8,128)(2,1)}) %all-gather.2.cloned.1.call-update) | async-done | bytes 4194320 | tf_op jit(solution)/shard_map/all_gather | solution.py:184
  93.3 101.0 %shard_map.136 = (f32[16,512,256]{2,1,0:T(8,128)}, f32[16,4,512,1]{3,2,1,0:T(8,128)}, f32[16,4,512,1]{3,2,1,0:T(8,128)}) custom-call(s32[34]{0:T(128)} %copy-done.14, s32[34]{0:T(128)} %get-tuple-element.62.page_ref, s32[34]{0:T(128)} %gather_fusion.2, s32[34]{0:T(128)} %gather_fusion.3, s32[34]{0:T(128)} %compare_convert_fusion.fresh_ref, ...), custom_call_target="tpu_custom_call" | custom-call | tf_op jit(solution)/shard_map/pallas_call | solution.py:109
  194.4 4.2 broadcast_select_fusion.2
  198.6 3.2 copy-done.1
  203.4 4.2 copy.114
  207.7 21.1 %broadcast_select_fusion.1 = (f32[16,4,512,1]{3,2,1,0:T(8,128)}, f32[16,4,512,1]{3,2,1,0:T(8,128)}) fusion(f32[16,4,512,1]{3,2,1,0:T(8,128)} %get-tuple-element.11, pred[16]{0:T(512)(128)(4,1)S(1)} %fusion.76, f32[16,4,512,1]{3,2,1,0:T(8,128)} %get-tuple-element.12), kind=kLoop, calls=%fused_computation.8 | loop fusion | flops 65536 | bytes 524304 | tf_op jit(solution)/shard_map/jit(_where)/select_n | solution.py:206
  228.8 10.0 %copy.95 = f32[16,4,512,1]{2,0,3,1:T(8,128)S(1)} copy(f32[16,4,512,1]{3,2,1,0:T(8,128)} %get-tuple-element.58) | data formatting | bytes 262144 | tf_op jit(solution)/shard_map/jit(_where)/select_n | solution.py:206
  238.8 10.0 %copy.96 = f32[16,4,512,1]{2,0,3,1:T(8,128)S(1)} copy(f32[16,4,512,1]{3,2,1,0:T(8,128)} %get-tuple-element.59) | data formatting | bytes 262144 | tf_op jit(solution)/shard_map/jit(_where)/select_n | solution.py:207
  251.7 4.6 constant_dynamic-slice_fusion.3
  256.3 5.2 %copy.94 = f32[2,2,2,2,2,1,128,256]{6,7,4,3,2,1,0,5:T(8,128)} copy(f32[2,2,2,2,2,1,128,256]{7,6,5,4,3,2,1,0:T(8,128)} %constant_dynamic-slice_fusion.3) | data formatting | bytes 8388608 | tf_op jit(solution)/shard_map/jit(dynamic_index_in_dim)/dynamic_slice | solution.py:221
  261.8 3.8 fusion
  268.1 2.5 collective-permute-done.4
  271.4 19.1 %collective-permute-done.3 = bf16[2,2,2,2,128,256]{4,5,3,2,1,0:T(8,128)(2,1)S(1)} collective-permute-done((bf16[2,2,2,2,128,256]{4,5,3,2,1,0:T(8,128)(2,1)S(1)}, bf16[2,2,2,2,128,256]{4,5,3,2,1,0:T(8,128)(2,1)S(1)}, u32[]{:S(2)}, u32[]{:S(2)}) %collective-permute-start.3) | collective-permute-done | bytes 1048608 | tf_op jit(solution)/shard_map/ppermute | solution.py:226
  291.2 2.6 collective-permute-start.8
  293.8 9.8 %collective-permute-done.5 = bf16[2,2,2,128,256]{3,4,2,1,0:T(8,128)(2,1)S(1)} collective-permute-done((bf16[2,2,2,128,256]{3,4,2,1,0:T(8,128)(2,1)S(1)}, bf16[2,2,2,128,256]{3,4,2,1,0:T(8,128)(2,1)S(1)}, u32[]{:S(2)}, u32[]{:S(2)}) %collective-permute-start.5) | collective-permute-done | bytes 524320 | tf_op jit(solution)/shard_map/ppermute | solution.py:226
  304.9 3.0 collective-permute-start.10
  307.9 3.4 collective-permute-done.7
  311.6 5.8 %collective-permute-done.9 = bf16[2,128,256]{1,2,0:T(8,128)(2,1)S(1)} collective-permute-done((bf16[2,128,256]{1,2,0:T(8,128)(2,1)S(1)}, bf16[2,128,256]{1,2,0:T(8,128)(2,1)S(1)}, u32[]{:S(2)}, u32[]{:S(2)}) %collective-permute-start.9) | collective-permute-done | bytes 131104 | tf_op jit(solution)/shard_map/ppermute | solution.py:226
  317.4 2.1 collective-permute-start.11
  319.5 5.7 %collective-permute-done.11 = bf16[128,256]{0,1:T(8,128)(2,1)S(1)} collective-permute-done((bf16[128,256]{0,1:T(8,128)(2,1)S(1)}, bf16[128,256]{0,1:T(8,128)(2,1)S(1)}, u32[]{:S(2)}, u32[]{:S(2)}) %collective-permute-start.11) | collective-permute-done | bytes 65568 | tf_op jit(solution)/shard_map/ppermute | solution.py:226
  326.6 2.4 collective-permute-start.13
  336.2 62.8 %all_to_all.10 = bf16[64,1,10,1024]{3,2,1,0:T(8,128)(2,1)S(1)} all-to-all(bf16[64,1,10,1024]{3,2,1,0:T(8,128)(2,1)S(1)} %bitcast.234), channel_id=1, replica_groups=mesh['seq'=64,'tp'=4] {'seq'}, dimensions={0} | all-to-all | bytes 2621440 | tf_op jit(solution)/shard_map/all_to_all | solution.py:279
  400.3 2.4 fusion.28
  404.9 2.1 copy.108
  407.1 7.1 %all-to-all-start.1 = ((bf16[64,1,10,1024]{3,2,1,0:T(8,128)(2,1)}), bf16[64,1,10,1024]{3,2,1,0:T(8,128)(2,1)S(1)}, u32[]{:S(2)}, u32[]{:S(2)}) async-start(bf16[64,1,10,1024]{3,2,1,0:T(8,128)(2,1)} %copy.108), calls=%async_computation.1 | async-start | bytes 4194304 | tf_op jit(solution)/shard_map/all_to_all | solution.py:291
  418.1 45.8 %all-to-all-done.1 = bf16[64,1,10,1024]{3,2,1,0:T(8,128)(2,1)S(1)} async-done(((bf16[64,1,10,1024]{3,2,1,0:T(8,128)(2,1)}), bf16[64,1,10,1024]{3,2,1,0:T(8,128)(2,1)S(1)}, u32[]{:S(2)}, u32[]{:S(2)}) %all-to-all-start.1) | async-done | bytes 1310752 | tf_op jit(solution)/shard_map/all_to_all | solution.py:291
  469.1 18.5 %reduce-scatter.2.cloned.1.call-done = bf16[128,256]{1,0:T(8,128)(2,1)} async-done(((bf16[128,1024]{1,0:T(8,128)(2,1)}), bf16[128,256]{1,0:T(8,128)(2,1)}) %reduce-scatter.2.cloned.1.call-update) | async-done | bytes 65552 | tf_op jit(solution)/shard_map/reduce_scatter | solution.py:301
  (160 shorter events, 52.1 us)
Async XLA Ops:
  6.5 397.5 %copy-start = (bf16[1,352,1024]{2,1,0:T(8,128)(2,1)S(1)}, bf16[1,352,1024]{2,1,0:T(8,128)(2,1)}, u32[]{:S(2)}) copy-start(bf16[1,352,1024]{2,1,0:T(8,128)(2,1)} %param.27) | copy-start | bytes 2162692
  6.5 20.3 %copy-start.2 = (bf16[128,1024]{1,0:T(8,128)(2,1)S(1)}, bf16[128,1024]{1,0:T(8,128)(2,1)}, u32[]{:S(2)}) copy-start(bf16[128,1024]{1,0:T(8,128)(2,1)} %param.14) | copy-start | bytes 786436
  6.5 20.3 %copy-start.13 = (s32[128,2]{0,1:T(2,128)S(1)}, s32[128,2]{0,1:T(2,128)}, u32[]{:S(2)}) copy-start(s32[128,2]{0,1:T(2,128)} %param.17) | copy-start | bytes 3076
  6.5 20.3 %copy-start.6 = (bf16[1024,256]{1,0:T(8,128)(2,1)S(1)}, bf16[1024,256]{1,0:T(8,128)(2,1)}, u32[]{:S(2)}) copy-start(bf16[1024,256]{1,0:T(8,128)(2,1)} %param.19) | copy-start | bytes 1572868
  6.5 86.8 %all-gather.2.cloned.1.call-start = ((), (), s32[]{:S(2)}) async-start(), calls=%async_computation.3 | async-start | bytes 4259840 | tf_op jit(solution)/shard_map/all_gather | solution.py:184
  9.8 18.0 %copy-start.7 = (bf16[1024,256]{1,0:T(8,128)(2,1)S(1)}, bf16[1024,256]{1,0:T(8,128)(2,1)}, u32[]{:S(2)}) copy-start(bf16[1024,256]{1,0:T(8,128)(2,1)} %param.20) | copy-start | bytes 1572868
  9.8 19.4 %collective-permute-start.15 = (bf16[256,1024]{1,0:T(8,128)(2,1)}, bf16[256,1024]{1,0:T(8,128)(2,1)S(1)}, u32[]{:S(2)}, u32[]{:S(2)}) collective-permute-start(bf16[256,1024]{1,0:T(8,128)(2,1)} %param.21), channel_id=1, source_target_pairs={{0,1},{1,2},{2,3},{3,0},{4,5},{5,6},{6,7},{7,4},{8,9},{9,10},{10,1... | collective-permute-start | bytes 1572872 | tf_op jit(solution)/shard_map/ppermute | solution.py:247
  12.0 25.5 %collective-permute-start.16 = (bf16[256,1024]{1,0:T(8,128)(2,1)}, bf16[256,1024]{1,0:T(8,128)(2,1)}, u32[]{:S(2)}, u32[]{:S(2)}) collective-permute-start(bf16[256,1024]{1,0:T(8,128)(2,1)} %param.21), channel_id=1, source_target_pairs={{0,2},{1,3},{2,0},{3,1},{4,6},{5,7},{6,4},{7,5},{8,10},{9,11},{10,... | collective-permute-start | bytes 1572872 | tf_op jit(solution)/shard_map/ppermute | solution.py:247
  14.7 22.9 %collective-permute-start.17 = (bf16[256,1024]{1,0:T(8,128)(2,1)}, bf16[256,1024]{1,0:T(8,128)(2,1)}, u32[]{:S(2)}, u32[]{:S(2)}) collective-permute-start(bf16[256,1024]{1,0:T(8,128)(2,1)} %param.21), channel_id=1, source_target_pairs={{0,3},{1,0},{2,1},{3,2},{4,7},{5,4},{6,5},{7,6},{8,11},{9,8},{10,9... | collective-permute-start | bytes 1572872 | tf_op jit(solution)/shard_map/ppermute | solution.py:247
  22.7 16.6 %copy-start.14 = (s32[34]{0:T(128)}, s32[34]{0:T(128)S(1)}, u32[]{:S(2)}) copy-start(s32[34]{0:T(128)S(1)} %gather_fusion) | copy-start | bytes 412
  29.2 8.3 %copy-start.8 = (bf16[256,1024]{1,0:T(8,128)(2,1)}, bf16[256,1024]{1,0:T(8,128)(2,1)S(1)}, u32[]{:S(2)}) copy-start(bf16[256,1024]{1,0:T(8,128)(2,1)S(1)} %collective-permute-done.15) | copy-start | bytes 1572868
  198.6 3.2 copy-start.1
  207.6 54.2 %collective-permute-start.1 = (bf16[2,2,2,2,2,128,256]{5,6,4,3,2,1,0:T(8,128)(2,1)}, bf16[2,2,2,2,2,128,256]{5,6,4,3,2,1,0:T(8,128)(2,1)}, u32[]{:S(2)}, u32[]{:S(2)}) collective-permute-start(bf16[2,2,2,2,2,128,256]{5,6,4,3,2,1,0:T(8,128)(2,1)} %bitcast.236), channel_id=1, source_target_pairs={{0,4},{4,0},{8,12},{12,8},{16,20},{20,16},{24,28},{28,24},{32,36},... | collective-permute-start | bytes 6291464 | tf_op jit(solution)/shard_map/ppermute | solution.py:226
  250.9 10.6 %collective-permute-start = (f32[2,2,2,2,2,128,4,2]{5,6,7,4,3,2,1,0:T(4,128)S(1)}, f32[2,2,2,2,2,128,4,2]{5,6,7,4,3,2,1,0:T(4,128)S(1)}, u32[]{:S(2)}, u32[]{:S(2)}) collective-permute-start(f32[2,2,2,2,2,128,4,2]{5,6,7,4,3,2,1,0:T(4,128)S(1)} %bitcast.243), channel_id=1, source_target_pairs={{0,4},{4,0},{8,12},{12,8},{16,20},{20,16},{24,28},{28,24},{32,36},... | collective-permute-start | bytes 393224 | tf_op jit(solution)/shard_map/ppermute | solution.py:227
  261.6 5.7 %collective-permute-start.2 = (f32[2,2,2,2,128,4,2]{4,5,6,3,2,1,0:T(4,128)S(1)}, f32[2,2,2,2,128,4,2]{4,5,6,3,2,1,0:T(4,128)S(1)}, u32[]{:S(2)}, u32[]{:S(2)}) collective-permute-start(f32[2,2,2,2,128,4,2]{4,5,6,3,2,1,0:T(4,128)S(1)} %get-tuple-element.36), channel_id=1, source_target_pairs={{0,8},{4,12},{8,0},{12,4},{16,24},{20,28},{24,16},{28,20},{32,40},... | collective-permute-start | bytes 196616 | tf_op jit(solution)/shard_map/ppermute | solution.py:227
  265.8 24.7 %collective-permute-start.3 = (bf16[2,2,2,2,128,256]{4,5,3,2,1,0:T(8,128)(2,1)S(1)}, bf16[2,2,2,2,128,256]{4,5,3,2,1,0:T(8,128)(2,1)S(1)}, u32[]{:S(2)}, u32[]{:S(2)}) collective-permute-start(bf16[2,2,2,2,128,256]{4,5,3,2,1,0:T(8,128)(2,1)S(1)} %fusion.17), channel_id=1, source_target_pairs={{0,8},{4,12},{8,0},{12,4},{16,24},{20,28},{24,16},{28,20},{32,40},... | collective-permute-start | bytes 3145736 | tf_op jit(solution)/shard_map/ppermute | solution.py:226
  267.4 3.1 collective-permute-start.4
  270.6 20.5 %collective-permute-start.6 = (f32[2,2,128,4,2]{2,3,4,1,0:T(4,128)S(1)}, f32[2,2,128,4,2]{2,3,4,1,0:T(4,128)S(1)}, u32[]{:S(2)}, u32[]{:S(2)}) collective-permute-start(f32[2,2,128,4,2]{2,3,4,1,0:T(4,128)S(1)} %get-tuple-element.42), channel_id=1, source_target_pairs={{0,16},{4,20},{8,24},{12,28},{16,0},{20,4},{24,8},{28,12},{32,48},... | collective-permute-start | bytes 49160 | tf_op jit(solution)/shard_map/ppermute | solution.py:227
  290.9 12.7 %collective-permute-start.5 = (bf16[2,2,2,128,256]{3,4,2,1,0:T(8,128)(2,1)S(1)}, bf16[2,2,2,128,256]{3,4,2,1,0:T(8,128)(2,1)S(1)}, u32[]{:S(2)}, u32[]{:S(2)}) collective-permute-start(bf16[2,2,2,128,256]{3,4,2,1,0:T(8,128)(2,1)S(1)} %fusion.34), channel_id=1, source_target_pairs={{0,32},{4,36},{8,40},{12,44},{16,48},{20,52},{24,56},{28,60},{32,0... | collective-permute-start | bytes 1572872 | tf_op jit(solution)/shard_map/ppermute | solution.py:226
  291.2 13.7 %collective-permute-start.8 = (f32[2,128,4,2]{1,2,3,0:T(4,128)S(1)}, f32[2,128,4,2]{1,2,3,0:T(4,128)S(1)}, u32[]{:S(2)}, u32[]{:S(2)}) collective-permute-start(f32[2,128,4,2]{1,2,3,0:T(4,128)S(1)} %get-tuple-element.46), channel_id=1, source_target_pairs={{0,64},{4,68},{8,72},{12,76},{16,80},{20,84},{24,88},{28,92},{32,9... | collective-permute-start | bytes 24584 | tf_op jit(solution)/shard_map/ppermute | solution.py:227
  303.8 7.5 %collective-permute-start.7 = (bf16[2,2,128,256]{2,3,1,0:T(8,128)(2,1)S(1)}, bf16[2,2,128,256]{2,3,1,0:T(8,128)(2,1)S(1)}, u32[]{:S(2)}, u32[]{:S(2)}) collective-permute-start(bf16[2,2,128,256]{2,3,1,0:T(8,128)(2,1)S(1)} %fusion.38), channel_id=1, source_target_pairs={{0,16},{4,20},{8,24},{12,28},{16,0},{20,4},{24,8},{28,12},{32,48},... | collective-permute-start | bytes 786440 | tf_op jit(solution)/shard_map/ppermute | solution.py:226
  304.9 14.6 %collective-permute-start.10 = (f32[128,4,2]{0,1,2:T(4,128)S(1)}, f32[128,4,2]{0,1,2:T(4,128)S(1)}, u32[]{:S(2)}, u32[]{:S(2)}) collective-permute-start(f32[128,4,2]{0,1,2:T(4,128)S(1)} %get-tuple-element.53), channel_id=1, source_target_pairs={{0,128},{4,132},{8,136},{12,140},{16,144},{20,148},{24,152},{28,15... | collective-permute-start | bytes 12296 | tf_op jit(solution)/shard_map/ppermute | solution.py:227
  311.4 5.9 %collective-permute-start.9 = (bf16[2,128,256]{1,2,0:T(8,128)(2,1)S(1)}, bf16[2,128,256]{1,2,0:T(8,128)(2,1)S(1)}, u32[]{:S(2)}, u32[]{:S(2)}) collective-permute-start(bf16[2,128,256]{1,2,0:T(8,128)(2,1)S(1)} %fusion.47), channel_id=1, source_target_pairs={{0,64},{4,68},{8,72},{12,76},{16,80},{20,84},{24,88},{28,92},{32,9... | collective-permute-start | bytes 393224 | tf_op jit(solution)/shard_map/ppermute | solution.py:226
  317.4 7.8 %collective-permute-start.11 = (bf16[128,256]{0,1:T(8,128)(2,1)S(1)}, bf16[128,256]{0,1:T(8,128)(2,1)S(1)}, u32[]{:S(2)}, u32[]{:S(2)}) collective-permute-start(bf16[128,256]{0,1:T(8,128)(2,1)S(1)} %fusion.50), channel_id=1, source_target_pairs={{0,128},{4,132},{8,136},{12,140},{16,144},{20,148},{24,152},{28,15... | collective-permute-start | bytes 196616 | tf_op jit(solution)/shard_map/ppermute | solution.py:226
  325.3 6.2 %collective-permute-start.12 = (bf16[128,256]{0,1:T(8,128)(2,1)S(1)}, bf16[128,256]{0,1:T(8,128)(2,1)S(1)}, u32[]{:S(2)}, u32[]{:S(2)}) collective-permute-start(bf16[128,256]{0,1:T(8,128)(2,1)S(1)} %fusion.48), channel_id=1, source_target_pairs={{0,1},{1,2},{2,3},{3,0},{4,5},{5,6},{6,7},{7,4},{8,9},{9,10},{10,1... | collective-permute-start | bytes 196616 | tf_op jit(solution)/shard_map/ppermute | solution.py:247
  326.6 5.0 %collective-permute-start.13 = (bf16[128,256]{0,1:T(8,128)(2,1)S(1)}, bf16[128,256]{0,1:T(8,128)(2,1)S(1)}, u32[]{:S(2)}, u32[]{:S(2)}) collective-permute-start(bf16[128,256]{0,1:T(8,128)(2,1)S(1)} %fusion.48), channel_id=1, source_target_pairs={{0,2},{1,3},{2,0},{3,1},{4,6},{5,7},{6,4},{7,5},{8,10},{9,11},{10,... | collective-permute-start | bytes 196616 | tf_op jit(solution)/shard_map/ppermute | solution.py:247
  329.0 3.1 collective-permute-start.14
  400.3 2.4 copy-start.5
  400.3 2.4 copy-start.15
  407.1 7.4 %copy-start.4 = (f32[128,1024]{1,0:T(8,128)S(1)}, f32[128,1024]{1,0:T(8,128)}, u32[]{:S(2)}) copy-start(f32[128,1024]{1,0:T(8,128)} %copy-done.3) | copy-start | bytes 1572868
  407.1 56.8 %all-to-all-start.1 = ((bf16[64,1,10,1024]{3,2,1,0:T(8,128)(2,1)}), bf16[64,1,10,1024]{3,2,1,0:T(8,128)(2,1)S(1)}, u32[]{:S(2)}, u32[]{:S(2)}) async-start(bf16[64,1,10,1024]{3,2,1,0:T(8,128)(2,1)} %copy.108), calls=%async_computation.1 | async-start | bytes 4194304 | tf_op jit(solution)/shard_map/all_to_all | solution.py:291
  414.2 73.5 %reduce-scatter.2.cloned.1.call-start = ((), (), s32[]{:S(2)}) async-start(), calls=%async_computation.4 | async-start | bytes 327680 | tf_op jit(solution)/shard_map/reduce_scatter | solution.py:301
  (5 other events, 7.3 us)
Sparse Core Ops, SparseCore 0:
  10.1 83.1 all-gather.1
  469.3 18.3 reduce-scatter.1
